TPU v7x, 256 devices: a whole 4x4x8 slice. The times are simulated.
256 devices in a mesh: blk: 64 (over z, x, core), head: 2 (over y_hi), dec: 2 (over y_lo).
Axes of the slice: x: 4, y: 4 (y_hi: 2, y_lo: 2; y = y_hi * 2 + y_lo), z: 8, core: 2. Of those that a mesh axis runs over, the one named last changes fastest.
Arguments:
- queries: bfloat16 [16384, 1536], P('blk', ('head', 'dec')), may hold values from -12 to 12
- key_vectors: bfloat16 [16384, 1536], P('blk', ('head', 'dec')), may hold values from -5 to 5
- values: bfloat16 [16384, 1536], P('blk', ('head', 'dec')), may hold values from -6 to 6
- lookback: int32 [12], replicated, may hold values from 0 to 5, as said below
- residual: bfloat16 [16384, 3072], P(('blk', 'head', 'dec')), may hold values from -0.1875 to 0.1875
- out_weight: bfloat16 [1536, 3072], P(('head', 'dec')), may hold values from -0.15625 to 0.15625
- branch_gate: float32 [3072], replicated, may hold values from 0.5 to 1.5
- final_shift: float32 [3072], replicated, may hold values from -0.5 to 0.5
- final_scale: float32 [3072], replicated, may hold values from -0.5 to 0.5
- final_weight: bfloat16 [3072, 64], replicated, may hold values from -0.109375 to 0.109375
- decoder_kernel: bfloat16 [432, 512], replicated, may hold values from -0.3125 to 0.3125
- decoder_bias: float32 [512], replicated, may hold values from -3 to 3
Outputs:
- features: bfloat16 [1024, 64, 512], P(('blk', 'head', 'dec'))
Inputs may be any that keep to these rules, and one draw needn't show every extreme that they name: lookback[h] is how many frames before its own the queries of head h may see; some head sees 5 earlier frames and some head none.
All inputs are finite; a program needn't handle non-finite values.
Results may differ from a plain program's by a relative error of at most 0.02.
Values may be sent and summed in bfloat16 or wider, within the bound.
No kernel may reach another device: no remote copies, remote signals or barrier semaphores. Data moves between devices by JAX's collectives and lax.ppermute only.
A program may use at most 192 MiB of HBM per device.

v0:
```python
import jax
import jax.numpy as jnp
from jax import lax
from jax.sharding import PartitionSpec as P

DH = 128
LC = 16
FRAMES = 8
PW = 32


def padded_2(cells, sides, width):
    for axis, dim in sides:
        count = lax.axis_size(axis)
        ends = count - 1
        head = lax.slice_in_dim(cells, 0, width, axis=dim)
        tail = lax.slice_in_dim(cells, cells.shape[dim] - width, cells.shape[dim], axis=dim)
        cells = jnp.concatenate(
            [
                lax.ppermute(tail, axis, [(i, (i + 1) % count) for i in range(ends)]),
                cells,
                lax.ppermute(head, axis, [((i + 1) % count, i) for i in range(ends)]),
            ],
            axis=dim,
        )
    return cells


def from_behind(x, axis, by):
    peers = lax.axis_size(axis)
    pairs = [(i, i + by) for i in range(peers) if 0 <= i + by < peers]
    return lax.ppermute(x, axis, pairs)


def attend_block(carry, shard_pair, query_heads, query_frame, lookback_heads, frame_len):
    running_max, row_total, accumulated = carry
    key_block, value_block = shard_pair
    key_count = key_block.shape[0]
    head_count = query_heads.shape[1]
    key_heads = key_block.reshape(key_count, head_count, DH)
    value_heads = value_block.reshape(key_count, head_count, DH)
    scores = jnp.einsum(
        "qhd,khd->hqk", query_heads, key_heads, preferred_element_type=jnp.float32
    ) * DH ** (-0.5)
    key_pos = jnp.arange(key_count, dtype=jnp.int32)
    key_frame = key_pos // frame_len
    visible = (
        (key_pos >= 0)[None, None, :]
        & (key_frame[None, None, :] <= query_frame[None, :, None])
        & (key_frame[None, None, :] >= query_frame[None, :, None] - lookback_heads[:, None, None])
    )
    masked = jnp.where(visible, scores, -1e30)
    newest_max = jnp.maximum(running_max, jnp.max(masked, axis=2))
    weights = jnp.where(visible, jnp.exp(scores - newest_max[:, :, None]), 0.0).astype(jnp.bfloat16)
    row_total = jnp.sum(weights.astype(jnp.float32), axis=2)
    accumulated = jnp.einsum(
        "hqk,khd->hqd", weights, value_heads, preferred_element_type=jnp.float32
    )
    return (newest_max, row_total, accumulated)


def per_device(
    queries,
    key_vectors,
    values,
    lookback,
    residual,
    out_weight,
    branch_gate,
    final_shift,
    final_scale,
    final_weight,
    decoder_kernel,
    decoder_bias,
):
    slab_rows = queries.shape[0]
    head_count = queries.shape[1] // DH
    blocks = lax.axis_size("blk")
    block_index = lax.axis_index("blk")
    frame_len = slab_rows * blocks // FRAMES
    query_heads = queries.reshape(slab_rows, head_count, DH)
    query_frame = (block_index * slab_rows + jnp.arange(slab_rows, dtype=jnp.int32)) // frame_len
    lookback_heads = lax.dynamic_slice_in_dim(
        lookback, lax.axis_index(("head", "dec")) * head_count, head_count
    )
    initial = (
        jnp.full((head_count, slab_rows), -1e30, jnp.float32),
        jnp.zeros((head_count, slab_rows), jnp.float32),
        jnp.zeros((head_count, slab_rows, DH), jnp.float32),
    )
    carry = attend_block(
        initial,
        (
            lax.all_gather(key_vectors, "blk", axis=0, tiled=True),
            lax.all_gather(values, "blk", axis=0, tiled=True),
        ),
        query_heads,
        query_frame,
        lookback_heads,
        frame_len,
    )
    newest_max, row_total, accumulated = carry
    attended = (
        (accumulated / row_total[:, :, None])
        .transpose(1, 0, 2)
        .reshape(slab_rows, head_count * DH)
        .astype(jnp.bfloat16)
    )
    tokens_dev = slab_rows // lax.axis_size(("head", "dec"))
    projected = lax.psum_scatter(
        jnp.dot(attended, out_weight, preferred_element_type=jnp.float32).astype(jnp.bfloat16),
        ("head", "dec"),
        scatter_dimension=0,
        tiled=True,
    ).astype(jnp.float32)
    hidden = residual.astype(jnp.float32) + branch_gate[None, :] * projected
    center = jnp.mean(hidden, axis=1, keepdims=True)
    spread = jnp.mean((hidden - center) ** 2, axis=1, keepdims=True)
    normed = (
        (hidden - center) * lax.rsqrt(spread + 1e-06) * (1.0 + final_scale[None, :])
        + final_shift[None, :]
    ).astype(jnp.bfloat16)
    patches = jnp.dot(normed, final_weight, preferred_element_type=jnp.float32).astype(jnp.bfloat16)
    patch_rows = tokens_dev // PW
    tile_rows = 2 * patch_rows
    width = 2 * PW
    tile = (
        patches.reshape(patch_rows, PW, 2, 2, LC)
        .transpose(0, 2, 1, 3, 4)
        .reshape(tile_rows, width * LC)
    )
    padded = padded_2(tile, ((("blk", "head", "dec"), 0),), 1)
    frame_stride = blocks // FRAMES
    frame_index = block_index // frame_stride
    prior_one = from_behind(padded, "blk", frame_stride)
    prior_one = jnp.where(frame_index >= 1, prior_one, padded)
    prior_two = from_behind(prior_one, "blk", frame_stride)
    prior_two = jnp.where(frame_index >= 1, prior_two, padded)
    history = jnp.stack([prior_two, prior_one, padded]).reshape(3, tile_rows + 2, width, LC)
    history = jnp.pad(history, ((0, 0), (0, 0), (1, 1), (0, 0)))
    windows = [
        history[time_tap, row_tap : row_tap + tile_rows, column_tap : column_tap + width, :]
        for time_tap in range(3)
        for row_tap in range(3)
        for column_tap in range(3)
    ]
    columns = jnp.concatenate(windows, axis=-1).reshape(tile_rows * width, 27 * LC)
    summed = (
        jnp.dot(columns, decoder_kernel, preferred_element_type=jnp.float32) + decoder_bias[None, :]
    )
    return summed.astype(jnp.bfloat16).reshape(tile_rows, width, decoder_kernel.shape[1])


def solution(mesh):
    in_specs = (
        P("blk", ("head", "dec")),
        P("blk", ("head", "dec")),
        P("blk", ("head", "dec")),
        P(),
        P(("blk", "head", "dec"), None),
        P(("head", "dec"), None),
        P(),
        P(),
        P(),
        P(),
        P(),
        P(),
    )
    out_specs = P(("blk", "head", "dec"), None, None)
    return jax.shard_map(
        per_device, mesh=mesh, in_specs=in_specs, out_specs=out_specs, check_vma=False
    )
```

profile of v0, /device:TPU:63, one launch (start us, length us, event | category | flops | bytes accessed | tf_op | source)
XLA Modules:
  0.0 313.7 jit_solution(12404184327450962504)
XLA Ops:
  6.5 1.9 copy.25
  8.5 0.7 all-gather.5.cloned.1.call-update
  9.3 1.1 copy.24
  10.3 0.7 dynamic_slice.3
  11.2 4.4 %broadcast_compare_fusion = pred[256,16384]{1,0:T(8,128)(4,1)} fusion(s32[16384]{0:T(1024)S(1)} %add_select_fusion, s32[256]{0:T(256)S(1)} %and_select_fusion), kind=kLoop, calls=%fused_computation.4 | loop fusion | flops 4194304 | bytes 4260864 | tf_op jit(solution)/shard_map/le | solution.py:49
  15.5 92.1 %all-gather.3.cloned.1.call-done = bf16[16384,384]{0,1:T(8,128)(2,1)} async-done(((bf16[256,384]{0,1:T(8,128)(2,1)}), bf16[16384,384]{0,1:T(8,128)(2,1)}) %all-gather.3.cloned.1.call-update) | async-done | bytes 12582928 | tf_op jit(solution)/shard_map/all_gather | solution.py:94
  107.6 29.0 %select_reduce_fusion = (f32[3,256]{1,0:T(4,128)S(1)}, f32[3,256,16384]{2,1,0:T(8,128)}) fusion(s32[3,256]{1,0:T(4,128)S(1)} %broadcast_subtract_fusion, s32[16384]{0:T(1024)S(1)} %add_select_fusion, pred[256,16384]{1,0:T(8,128)(4,1)} %broadcast_compare_fusion, bf16[256,3,128]{0,2,1:T(8,128)(2,1)S(1)} %bitcast.81, bf16[16384,3,128]{0,2,1:T(8,128)(2,1)} %bitcast.84), kind=kOutput, calls=%fused_computation.2 | convolution fusion | flops 3284139264 | bytes 67377152 | tf_op jit(solution)/shard_map/qhd,khd->hqk/dot_general | solution.py:42
  136.6 25.4 %convert_reduce_fusion = f32[3,256]{1,0:T(4,128)S(1)} fusion(f32[3,256]{1,0:T(4,128)S(1)} %broadcast_maximum_fusion, f32[3,256,16384]{2,1,0:T(8,128)} %get-tuple-element.34, s32[3,256]{1,0:T(4,128)S(1)} %broadcast_subtract_fusion, s32[16384]{0:T(1024)S(1)} %add_select_fusion, pred[256,16384]{1,0:T(8,128)(4,1)} %broadcast_compare_fusion), kind=kLoop, calls=%fused_computation | loop fusion | flops 100662528 | bytes 54600704 | tf_op jit(solution)/shard_map/reduce_sum | solution.py:55
  162.0 36.5 %all-gather.5.cloned.1.call-done = bf16[16384,384]{1,0:T(8,128)(2,1)} async-done(((bf16[256,384]{1,0:T(8,128)(2,1)}), bf16[16384,384]{1,0:T(8,128)(2,1)}) %all-gather.5.cloned.1.call-update) | async-done | bytes 12582928 | tf_op jit(solution)/shard_map/all_gather | solution.py:95
  198.6 16.7 %copy.28 = bf16[16384,384]{0,1:T(8,128)(2,1)} copy(bf16[16384,384]{1,0:T(8,128)(2,1)} %all-gather.5.cloned.1.call-done) | data formatting | bytes 25165824 | tf_op jit(solution)/shard_map/all_gather | solution.py:95
  215.3 24.8 %fusion.2 = bf16[256,3,128]{0,2,1:T(8,128)(2,1)S(1)} fusion(bf16[16384,3,128]{0,2,1:T(8,128)(2,1)} %bitcast.51, f32[256,3]{0,1:T(4,128)S(1)} %bitcast.83, f32[3,256,16384]{2,1,0:T(8,128)} %get-tuple-element.34, f32[3,256]{1,0:T(4,128)S(1)} %broadcast_maximum_fusion, s32[3,256]{1,0:T(4,128)S(1)} %broadcast_subtract_fusion, s32[16384]{0:T(1024)S(1)} %add_select_fusion, ...), kind=kOutput, calls=%fused_computation.10 | convolution fusion | flops 3296919552 | bytes 67380224 | tf_op jit(solution)/shard_map/hqk,khd->hqd/dot_general | solution.py:56
  240.2 2.2 convolution_convert_fusion
  242.4 25.2 %reduce-scatter.2.cloned.1.call-done = bf16[64,3072]{1,0:T(8,128)(2,1)} async-done(((bf16[256,3072]{1,0:T(8,128)(2,1)}), bf16[64,3072]{1,0:T(8,128)(2,1)}) %reduce-scatter.2.cloned.1.call-update) | async-done | bytes 393232 | tf_op jit(solution)/shard_map/reduce_scatter | solution.py:110
  267.6 1.2 fusion.3
  268.8 1.3 multiply_reduce_fusion
  270.1 1.4 convolution_convert_fusion.1
  271.7 0.1 copy.30
  271.8 0.1 reshape.177
  272.0 5.3 %collective-permute-start = (bf16[1,1024]{1,0:T(2,128)(2,1)S(1)}, bf16[1,1024]{1,0:T(2,128)(2,1)S(1)}, u32[]{:S(2)}, u32[]{:S(2)}) collective-permute-start(bf16[1,1024]{1,0:T(2,128)(2,1)S(1)} %get-tuple-element.31), channel_id=1, source_target_pairs={{0,1},{1,2},{2,3},{3,4},{4,5},{5,6},{6,7},{7,8},{8,9},{9,10},{10,1... | collective-permute-start | bytes 6152 | tf_op jit(solution)/shard_map/ppermute | solution.py:20
  277.3 1.9 collective-permute-start.1
  279.5 6.9 %collective-permute-done.1 = bf16[1,1024]{1,0:T(2,128)(2,1)S(1)} collective-permute-done((bf16[1,1024]{1,0:T(2,128)(2,1)S(1)}, bf16[1,1024]{1,0:T(2,128)(2,1)S(1)}, u32[]{:S(2)}, u32[]{:S(2)}) %collective-permute-start.1) | collective-permute-done | bytes 2080 | tf_op jit(solution)/shard_map/ppermute | solution.py:22
  286.7 3.2 %collective-permute-start.2 = (bf16[6,1024]{1,0:T(8,128)(2,1)S(1)}, bf16[6,1024]{1,0:T(8,128)(2,1)S(1)}, u32[]{:S(2)}, u32[]{:S(2)}) collective-permute-start(bf16[6,1024]{1,0:T(8,128)(2,1)S(1)} %pad_maximum_fusion.2), channel_id=1, source_target_pairs={{0,32},{4,36},{8,40},{12,44},{16,48},{20,52},{24,56},{28,60},{32,6... | collective-permute-start | bytes 36872 | tf_op jit(solution)/shard_map/ppermute | solution.py:32
  289.9 0.1 copy.52
  290.1 1.1 collective-permute-done.2
  291.2 5.1 %collective-permute-start.3 = (bf16[6,1024]{1,0:T(8,128)(2,1)S(1)}, bf16[6,1024]{1,0:T(8,128)(2,1)S(1)}, u32[]{:S(2)}, u32[]{:S(2)}) collective-permute-start(bf16[6,1024]{1,0:T(8,128)(2,1)S(1)} %broadcast_select_fusion.1), channel_id=1, source_target_pairs={{0,32},{4,36},{8,40},{12,44},{16,48},{20,52},{24,56},{28,60},{32,6... | collective-permute-start | bytes 36872 | tf_op jit(solution)/shard_map/ppermute | solution.py:32
  296.3 0.1 stack.11
  296.4 0.7 fusion.17
  297.3 0.1 stack.10
  297.5 0.7 fusion.18
  298.3 0.1 fusion.19
  298.4 0.1 copy.38
  298.5 0.1 copy.39
  298.6 0.1 copy.40
  298.8 0.1 copy.41
  298.9 0.1 copy.42
  299.0 0.1 copy.43
  299.1 0.1 copy.44
  299.2 0.1 copy.45
  299.3 0.1 copy.46
  299.4 0.1 copy.47
  299.5 0.1 copy.48
  299.7 0.1 copy.53
  299.9 0.7 copy.56
  300.7 0.7 copy.57
  301.4 0.7 copy.61
  302.1 0.7 copy.37
  302.8 2.2 concatenate.111
  305.1 2.1 fusion
  (46 shorter events, 1.6 us)
Async XLA Ops:
  6.5 233.6 %copy-start = (bf16[384,3072]{1,0:T(8,128)(2,1)S(1)}, bf16[384,3072]{1,0:T(8,128)(2,1)}, u32[]{:S(2)}) copy-start(bf16[384,3072]{1,0:T(8,128)(2,1)} %param.17) | copy-start | bytes 7077892
  6.5 101.1 %all-gather.3.cloned.1.call-start = ((), (), s32[]{:S(2)}) async-start(), calls=%async_computation.1 | async-start | bytes 12779520 | tf_op jit(solution)/shard_map/all_gather | solution.py:94
  8.5 190.1 %all-gather.5.cloned.1.call-start = ((), (), s32[]{:S(2)}) async-start(), calls=%async_computation.2 | async-start | bytes 12779520 | tf_op jit(solution)/shard_map/all_gather | solution.py:95
  9.2 258.3 %reduce-scatter.2.cloned.1.call-start = ((), (), s32[]{:S(2)}) async-start(), calls=%async_computation.3 | async-start | bytes 1966080 | tf_op jit(solution)/shard_map/reduce_scatter | solution.py:110
  215.3 27.1 %copy-start.3 = (f32[3072]{0:T(1024)S(1)}, f32[3072]{0:T(1024)}, u32[]{:S(2)}) copy-start(f32[3072]{0:T(1024)} %param.20) | copy-start | bytes 36868
  215.3 52.3 %copy-start.1 = (bf16[64,3072]{1,0:T(8,128)(2,1)S(1)}, bf16[64,3072]{1,0:T(8,128)(2,1)}, u32[]{:S(2)}) copy-start(bf16[64,3072]{1,0:T(8,128)(2,1)} %param.16) | copy-start | bytes 1179652
  215.3 52.3 %copy-start.2 = (f32[3072]{0:T(1024)S(1)}, f32[3072]{0:T(1024)}, u32[]{:S(2)}) copy-start(f32[3072]{0:T(1024)} %param.18) | copy-start | bytes 36868
  215.3 54.8 %copy-start.4 = (bf16[3072,64]{0,1:T(8,128)(2,1)S(1)}, bf16[3072,64]{0,1:T(8,128)(2,1)}, u32[]{:S(2)}) copy-start(bf16[3072,64]{0,1:T(8,128)(2,1)} %param.21) | copy-start | bytes 1179652
  215.3 54.8 %copy-start.5 = (f32[3072]{0:T(1024)S(1)}, f32[3072]{0:T(1024)}, u32[]{:S(2)}) copy-start(f32[3072]{0:T(1024)} %param.19) | copy-start | bytes 36868
  272.0 7.4 %collective-permute-start = (bf16[1,1024]{1,0:T(2,128)(2,1)S(1)}, bf16[1,1024]{1,0:T(2,128)(2,1)S(1)}, u32[]{:S(2)}, u32[]{:S(2)}) collective-permute-start(bf16[1,1024]{1,0:T(2,128)(2,1)S(1)} %get-tuple-element.31), channel_id=1, source_target_pairs={{0,1},{1,2},{2,3},{3,4},{4,5},{5,6},{6,7},{7,8},{8,9},{9,10},{10,1... | collective-permute-start | bytes 6152 | tf_op jit(solution)/shard_map/ppermute | solution.py:20
  277.3 9.1 %collective-permute-start.1 = (bf16[1,1024]{1,0:T(2,128)(2,1)S(1)}, bf16[1,1024]{1,0:T(2,128)(2,1)S(1)}, u32[]{:S(2)}, u32[]{:S(2)}) collective-permute-start(bf16[1,1024]{1,0:T(2,128)(2,1)S(1)} %get-tuple-element.32), channel_id=1, source_target_pairs={{1,0},{2,1},{3,2},{4,3},{5,4},{6,5},{7,6},{8,7},{9,8},{10,9},{11,1... | collective-permute-start | bytes 6152 | tf_op jit(solution)/shard_map/ppermute | solution.py:22
  286.7 4.5 %collective-permute-start.2 = (bf16[6,1024]{1,0:T(8,128)(2,1)S(1)}, bf16[6,1024]{1,0:T(8,128)(2,1)S(1)}, u32[]{:S(2)}, u32[]{:S(2)}) collective-permute-start(bf16[6,1024]{1,0:T(8,128)(2,1)S(1)} %pad_maximum_fusion.2), channel_id=1, source_target_pairs={{0,32},{4,36},{8,40},{12,44},{16,48},{20,52},{24,56},{28,60},{32,6... | collective-permute-start | bytes 36872 | tf_op jit(solution)/shard_map/ppermute | solution.py:32
  291.2 6.1 %collective-permute-start.3 = (bf16[6,1024]{1,0:T(8,128)(2,1)S(1)}, bf16[6,1024]{1,0:T(8,128)(2,1)S(1)}, u32[]{:S(2)}, u32[]{:S(2)}) collective-permute-start(bf16[6,1024]{1,0:T(8,128)(2,1)S(1)} %broadcast_select_fusion.1), channel_id=1, source_target_pairs={{0,32},{4,36},{8,40},{12,44},{16,48},{20,52},{24,56},{28,60},{32,6... | collective-permute-start | bytes 36872 | tf_op jit(solution)/shard_map/ppermute | solution.py:32
Sparse Core Ops, SparseCore 0:
  10.0 97.6 all-gather.2
  110.4 88.1 all-gather.4
  242.5 25.0 reduce-scatter.1
where the time goes:
time: 316 us; the launch traced here: 314 us
  waiting for transfers between devices  163 us (52%)
  matrix products  59.5 us (19%)
  other arithmetic  32.6 us (10%)
  local copies, waits for them, and re-layouts  30 us (9%)
  starting transfers between devices  15.6 us (5%)
  between operations  13.4 us (4%)
    all_gather x1, waiting for transfers between devices, per_device(): lax.all_gather(key_vectors, 'blk', axis=0, tiled=True)  92.1 us
    all_gather x1, waiting for transfers between devices, per_device(): lax.all_gather(values, 'blk', axis=0, tiled=True)  36.5 us
    dot_general x1, matrix products, attend_block(): jnp.einsum('qhd,khd->hqk', query_heads, key_heads, preferred_element_type...  29 us
    reduce_sum x1, other arithmetic, attend_block(): row_total = jnp.sum(weights.astype(jnp.float32), axis=2)  25.4 us
    reduce_scatter x1, waiting for transfers between devices, per_device(): lax.psum_scatter(jnp.dot(attended, out_weight, preferred_element_type=jnp...  25.2 us
    dot_general x1, matrix products, attend_block(): jnp.einsum('hqk,khd->hqd', weights, value_heads, preferred_element_type=j...  24.8 us
    all_gather x1, local copies, waits for them, and re-layouts, per_device(): lax.all_gather(values, 'blk', axis=0, tiled=True)  16.7 us
    ppermute x2, starting transfers between devices, from_behind(): return lax.ppermute(x, axis, pairs)  8.3 us
  transfers between devices with their start and end apart: 7, of which 5 were waited for; matrix products, arithmetic and copies ran while one was open for 20% of the time, Pallas kernels for 0%

commit v1 on v0

v1 whole, which is shorter than its diff:
```python
import functools

import jax
import jax.numpy as jnp
from jax import lax
from jax.experimental import pallas as pl
from jax.experimental.pallas import tpu as pltpu
from jax.sharding import Mesh
from jax.sharding import PartitionSpec as P

DH = 128
LC = 16
FRAMES = 8
PW = 32

ROWS = ("z", "x", "core", "head", "dec")


def padded_2(cells, sides, width):
    for axis, dim in sides:
        count = lax.axis_size(axis)
        ends = count - 1
        head = lax.slice_in_dim(cells, 0, width, axis=dim)
        tail = lax.slice_in_dim(cells, cells.shape[dim] - width, cells.shape[dim], axis=dim)
        cells = jnp.concatenate(
            [
                lax.ppermute(tail, axis, [(i, (i + 1) % count) for i in range(ends)]),
                cells,
                lax.ppermute(head, axis, [((i + 1) % count, i) for i in range(ends)]),
            ],
            axis=dim,
        )
    return cells


def from_behind(x, axis, by):
    peers = lax.axis_size(axis)
    pairs = [(i, i + by) for i in range(peers) if 0 <= i + by < peers]
    return lax.ppermute(x, axis, pairs)


def attend_kernel(head_count, part_rows, sp_ref, q_ref, kv_ref, o_ref, m_sc, l_sc, acc_sc):
    step = pl.program_id(0)
    frame_now = sp_ref[0]
    first = sp_ref[1]
    frame = first + step
    hd = head_count * DH

    @pl.when(step == 0)
    def _():
        m_sc[...] = jnp.full(m_sc.shape, -1e30, jnp.float32)
        l_sc[...] = jnp.zeros(l_sc.shape, jnp.float32)
        acc_sc[...] = jnp.zeros(acc_sc.shape, jnp.float32)

    for h in range(head_count):
        seen = (frame <= frame_now) & (frame >= frame_now - sp_ref[2 + h])

        @pl.when(seen)
        def _():
            q = q_ref[:, h * DH:(h + 1) * DH]
            for c in range(kv_ref.shape[0]):
                k = kv_ref[c, :, h * DH:(h + 1) * DH]
                v = kv_ref[c, :, hd + h * DH:hd + (h + 1) * DH]
                s = lax.dot_general(
                    q, k, (((1,), (1,)), ((), ())), preferred_element_type=jnp.float32
                ) * DH ** (-0.5)
                m_old = m_sc[h]
                m_new = jnp.maximum(m_old, jnp.max(s, axis=1, keepdims=True))
                alpha = jnp.exp(m_old - m_new)
                p = jnp.exp(s - m_new).astype(jnp.bfloat16)
                l_sc[h] = alpha * l_sc[h] + jnp.sum(p.astype(jnp.float32), axis=1, keepdims=True)
                acc_sc[h] = alpha * acc_sc[h] + jnp.dot(p, v, preferred_element_type=jnp.float32)
                m_sc[h] = m_new

    @pl.when(step == pl.num_programs(0) - 1)
    def _():
        for h in range(head_count):
            o_ref[:, h * DH:(h + 1) * DH] = (acc_sc[h] / l_sc[h]).astype(o_ref.dtype)


def attend(scalars, queries, kv):
    parts, frames, part_rows, width = kv.shape
    rows, hd = queries.shape
    head_count = hd // DH

    def kv_map(step, sp):
        return (0, jnp.minimum(sp[1] + step, sp[0]), 0, 0)

    flops = 4 * rows * parts * part_rows * hd * 6
    return pl.pallas_call(
        functools.partial(attend_kernel, head_count, part_rows),
        out_shape=jax.ShapeDtypeStruct((rows, hd), jnp.bfloat16),
        grid_spec=pltpu.PrefetchScalarGridSpec(
            num_scalar_prefetch=1,
            grid=(frames,),
            in_specs=[
                pl.BlockSpec((rows, hd), lambda step, sp: (0, 0)),
                pl.BlockSpec((parts, None, part_rows, width), kv_map),
            ],
            out_specs=pl.BlockSpec((rows, hd), lambda step, sp: (0, 0)),
            scratch_shapes=[
                pltpu.VMEM((head_count, rows, 1), jnp.float32),
                pltpu.VMEM((head_count, rows, 1), jnp.float32),
                pltpu.VMEM((head_count, rows, DH), jnp.float32),
            ],
        ),
        compiler_params=pltpu.CompilerParams(
            dimension_semantics=("arbitrary",), vmem_limit_bytes=48 * 1024 * 1024
        ),
        cost_estimate=pl.CostEstimate(
            flops=flops,
            transcendentals=rows * parts * part_rows * head_count * 6,
            bytes_accessed=parts * part_rows * width * 2 * 6 + rows * hd * 4,
        ),
    )(scalars, queries, kv)


def per_device(
    queries,
    key_vectors,
    values,
    lookback,
    residual,
    out_weight,
    branch_gate,
    final_shift,
    final_scale,
    final_weight,
    decoder_kernel,
    decoder_bias,
):
    slab_rows = queries.shape[0]
    head_count = queries.shape[1] // DH
    frame_index = lax.axis_index("z")
    lookback_heads = lax.dynamic_slice_in_dim(
        lookback, lax.axis_index(("head", "dec")) * head_count, head_count
    )
    first_frame = jnp.maximum(frame_index - jnp.max(lookback_heads), 0)
    scalars = jnp.concatenate(
        [jnp.stack([frame_index, first_frame]).astype(jnp.int32), lookback_heads.astype(jnp.int32)]
    )

    kv = jnp.concatenate([key_vectors, values], axis=1)
    kv = lax.all_gather(kv, ("z", "x"), axis=0, tiled=True)
    kv = lax.all_gather(kv, "core", axis=0, tiled=False)
    parts = kv.shape[0]
    kv = kv.reshape(parts, FRAMES, kv.shape[1] // FRAMES, kv.shape[2])
    attended = attend(scalars, queries, kv)

    tokens_dev = slab_rows // lax.axis_size(("head", "dec"))
    projected = lax.psum_scatter(
        jnp.dot(attended, out_weight, preferred_element_type=jnp.float32).astype(jnp.bfloat16),
        ("head", "dec"),
        scatter_dimension=0,
        tiled=True,
    ).astype(jnp.float32)
    hidden = residual.astype(jnp.float32) + branch_gate[None, :] * projected
    center = jnp.mean(hidden, axis=1, keepdims=True)
    spread = jnp.mean((hidden - center) ** 2, axis=1, keepdims=True)
    normed = (
        (hidden - center) * lax.rsqrt(spread + 1e-06) * (1.0 + final_scale[None, :])
        + final_shift[None, :]
    ).astype(jnp.bfloat16)
    patches = jnp.dot(normed, final_weight, preferred_element_type=jnp.float32).astype(jnp.bfloat16)
    patch_rows = tokens_dev // PW
    tile_rows = 2 * patch_rows
    width = 2 * PW
    tile = (
        patches.reshape(patch_rows, PW, 2, 2, LC)
        .transpose(0, 2, 1, 3, 4)
        .reshape(tile_rows, width * LC)
    )
    padded = padded_2(tile, ((ROWS, 0),), 1)
    prior_one = from_behind(padded, "z", 1)
    prior_one = jnp.where(frame_index >= 1, prior_one, padded)
    prior_two = from_behind(prior_one, "z", 1)
    prior_two = jnp.where(frame_index >= 1, prior_two, padded)
    history = jnp.stack([prior_two, prior_one, padded]).reshape(3, tile_rows + 2, width, LC)
    history = jnp.pad(history, ((0, 0), (0, 0), (1, 1), (0, 0)))
    windows = [
        history[time_tap, row_tap : row_tap + tile_rows, column_tap : column_tap + width, :]
        for time_tap in range(3)
        for row_tap in range(3)
        for column_tap in range(3)
    ]
    columns = jnp.concatenate(windows, axis=-1).reshape(tile_rows * width, 27 * LC)
    summed = (
        jnp.dot(columns, decoder_kernel, preferred_element_type=jnp.float32) + decoder_bias[None, :]
    )
    return summed.astype(jnp.bfloat16).reshape(tile_rows, width, decoder_kernel.shape[1])


def solution(mesh):
    blocks = mesh.shape["blk"]
    fine = Mesh(
        mesh.devices.reshape(FRAMES, blocks // FRAMES // 2, 2, mesh.shape["head"], mesh.shape["dec"]),
        ROWS,
    )
    rows = ("z", "x", "core")
    in_specs = (
        P(rows, ("head", "dec")),
        P(rows, ("head", "dec")),
        P(rows, ("head", "dec")),
        P(),
        P(ROWS, None),
        P(("head", "dec"), None),
        P(),
        P(),
        P(),
        P(),
        P(),
        P(),
    )
    out_specs = P(ROWS, None, None)
    return jax.shard_map(
        per_device, mesh=fine, in_specs=in_specs, out_specs=out_specs, check_vma=False
    )
```

time: 316 us -> 282 us (0.89)
  matrix products: 59.5 us -> 5.59 us
  waiting for transfers between devices: 163 us -> 214 us
  other arithmetic: 32.6 us -> 5.47 us
  local copies, waits for them, and re-layouts: 30 us -> 12.3 us
  Pallas kernels: 0 us -> 11.8 us
    dot_general x2 -> x0, matrix products: 53.8 us -> none  [the longest x1 29 us: attend_block(): jnp.einsum('qhd,khd->hqk', query_heads, key_heads, preferred_element_type...]
    all_gather x2, waiting for transfers between devices: 129 us -> 165 us  [the longest x1 118 us: per_device(): kv = lax.all_gather(kv, ('z', 'x'), axis=0, tiled=True)]
    reduce_sum x1 -> x0, other arithmetic: 25.4 us -> none  [attend_block(): row_total = jnp.sum(weights.astype(jnp.float32), axis=2)]
    all_gather x1 -> x0, local copies, waits for them, and re-layouts: 16.7 us -> none  [per_device(): lax.all_gather(values, 'blk', axis=0, tiled=True)]
    reduce_scatter x1, waiting for transfers between devices: 25.2 us -> 40.8 us  [per_device(): lax.psum_scatter(jnp.dot(attended, out_weight, preferred_element_type=jnp...]
    pallas_call x0 -> x1, Pallas kernels: none -> 11.8 us  [attend(): pl.pallas_call(functools.partial(attend_kernel, head_count, part_rows), o...]
    le x1 -> x0, other arithmetic: 4.36 us -> none  [attend_block(): key_frame[None, None, :] <= query_frame[None, :, None]]
  transfers between devices with their start and end apart: 7 -> 7, of which waited for: 5 -> 5; matrix products, arithmetic and copies ran while one was open for 20% -> 1% of each run, Pallas kernels for 0% -> 0%
where the time goes in v1:
time: 282 us; the launch traced here: 279 us
  waiting for transfers between devices  214 us (76%)
  starting transfers between devices  15.6 us (6%)
  between operations  14 us (5%)
  local copies, waits for them, and re-layouts  12.3 us (4%)
  Pallas kernels  11.8 us (4%)
  matrix products  5.59 us (2%)
  other arithmetic  5.47 us (2%)
    all_gather x1, waiting for transfers between devices, per_device(): kv = lax.all_gather(kv, ('z', 'x'), axis=0, tiled=True)  118 us
    all_gather x1, waiting for transfers between devices, per_device(): kv = lax.all_gather(kv, 'core', axis=0, tiled=False)  47.3 us
    reduce_scatter x1, waiting for transfers between devices, per_device(): lax.psum_scatter(jnp.dot(attended, out_weight, preferred_element_type=jnp...  40.8 us
    pallas_call x1, Pallas kernels, attend(): pl.pallas_call(functools.partial(attend_kernel, head_count, part_rows), o...  11.8 us
    ppermute x2, starting transfers between devices, from_behind(): return lax.ppermute(x, axis, pairs)  8.28 us
    slice x23, local copies, waits for them, and re-layouts, per_device(): history[time_tap, row_tap:row_tap + tile_rows, column_tap:column_tap + wi...  8.21 us
    ppermute x1, waiting for transfers between devices, padded_2(): lax.ppermute(head, axis, [((i + 1) % count, i) for i in range(ends)])  6.94 us
  transfers between devices with their start and end apart: 7, of which 5 were waited for; matrix products, arithmetic and copies ran while one was open for 1% of the time, Pallas kernels for 0%

profile of v1, /device:TPU:63, one launch (start us, length us, event | category | flops | bytes accessed | tf_op | source)
XLA Modules:
  0.0 278.8 jit_solution(17123589883096770709)
XLA Ops:
  6.5 1.9 pad_maximum_fusion
  8.6 118.0 %all-gather.4.cloned.1.call-done = bf16[8192,768]{1,0:T(8,128)(2,1)} async-done(((bf16[256,768]{1,0:T(8,128)(2,1)}), bf16[8192,768]{1,0:T(8,128)(2,1)}) %all-gather.4.cloned.1.call-update) | async-done | bytes 12582928 | tf_op jit(solution)/shard_map/all_gather | solution.py:144
  126.7 0.6 copy-done.5
  127.2 0.7 fusion.12
  128.7 47.3 %all-gather.6.cloned.1.call-done = bf16[16384,768]{1,0:T(8,128)(2,1)} async-done(((bf16[8192,768]{1,0:T(8,128)(2,1)}), bf16[16384,768]{1,0:T(8,128)(2,1)}) %all-gather.6.cloned.1.call-update) | async-done | bytes 25165840 | tf_op jit(solution)/shard_map/all_gather | solution.py:145
  175.9 11.8 %shard_map.118 = bf16[256,384]{1,0:T(8,128)(2,1)S(1)} custom-call(s32[5]{0:T(128)S(1)} %pad_add_fusion.sp_ref, bf16[256,384]{1,0:T(8,128)(2,1)S(1)} %copy-done.1, bf16[2,8,1024,768]{3,2,1,0:T(8,128)(2,1)} %bitcast.40), custom_call_target="tpu_custom_call" | custom-call | flops 4831838208 | bytes 19267584 | tf_op jit(solution)/shard_map/pallas_call | solution.py:90
  187.7 2.1 convolution_convert_fusion
  189.9 40.8 %reduce-scatter.2.cloned.1.call-done = bf16[64,3072]{1,0:T(8,128)(2,1)} async-done(((bf16[256,3072]{1,0:T(8,128)(2,1)}), bf16[64,3072]{1,0:T(8,128)(2,1)}) %reduce-scatter.2.cloned.1.call-update) | async-done | bytes 393232 | tf_op jit(solution)/shard_map/reduce_scatter | solution.py:151
  230.7 1.2 fusion.1
  231.9 1.3 multiply_reduce_fusion
  233.3 1.4 convolution_convert_fusion.1
  234.8 0.1 copy.18
  234.9 0.1 reshape.98
  235.1 5.3 %collective-permute-start = (bf16[1,1024]{1,0:T(2,128)(2,1)S(1)}, bf16[1,1024]{1,0:T(2,128)(2,1)S(1)}, u32[]{:S(2)}, u32[]{:S(2)}) collective-permute-start(bf16[1,1024]{1,0:T(2,128)(2,1)S(1)} %get-tuple-element.33), channel_id=1, source_target_pairs={{0,1},{1,2},{2,3},{3,4},{4,5},{5,6},{6,7},{7,8},{8,9},{9,10},{10,1... | collective-permute-start | bytes 6152 | tf_op jit(solution)/shard_map/ppermute | solution.py:27
  240.4 1.9 collective-permute-start.1
  242.6 6.9 %collective-permute-done.1 = bf16[1,1024]{1,0:T(2,128)(2,1)S(1)} collective-permute-done((bf16[1,1024]{1,0:T(2,128)(2,1)S(1)}, bf16[1,1024]{1,0:T(2,128)(2,1)S(1)}, u32[]{:S(2)}, u32[]{:S(2)}) %collective-permute-start.1) | collective-permute-done | bytes 2080 | tf_op jit(solution)/shard_map/ppermute | solution.py:29
  249.8 3.2 %collective-permute-start.2 = (bf16[6,1024]{1,0:T(8,128)(2,1)S(1)}, bf16[6,1024]{1,0:T(8,128)(2,1)S(1)}, u32[]{:S(2)}, u32[]{:S(2)}) collective-permute-start(bf16[6,1024]{1,0:T(8,128)(2,1)S(1)} %pad_maximum_fusion.3), channel_id=1, source_target_pairs={{0,32},{32,64},{64,96},{96,128},{128,160},{160,192},{192,224},{1,3... | collective-permute-start | bytes 36872 | tf_op jit(solution)/shard_map/ppermute | solution.py:39
  252.9 0.1 copy.40
  253.0 0.1 copy.48
  253.1 1.1 collective-permute-done.2
  254.3 5.1 %collective-permute-start.3 = (bf16[6,1024]{1,0:T(8,128)(2,1)S(1)}, bf16[6,1024]{1,0:T(8,128)(2,1)S(1)}, u32[]{:S(2)}, u32[]{:S(2)}) collective-permute-start(bf16[6,1024]{1,0:T(8,128)(2,1)S(1)} %broadcast_select_fusion.1), channel_id=1, source_target_pairs={{0,32},{32,64},{64,96},{96,128},{128,160},{160,192},{192,224},{1,3... | collective-permute-start | bytes 36872 | tf_op jit(solution)/shard_map/ppermute | solution.py:39
  259.4 0.1 stack.19
  259.5 0.7 fusion.13
  260.4 0.1 stack.18
  260.5 0.1 copy.23
  260.6 0.7 fusion.14
  261.3 0.1 fusion.8
  261.4 0.7 fusion.15
  262.1 0.1 copy.28
  262.2 0.1 copy.29
  262.3 0.1 copy.30
  262.4 0.1 copy.31
  262.5 0.1 copy.32
  262.7 0.1 copy.33
  262.8 0.1 copy.34
  262.9 0.1 copy.35
  263.0 0.1 copy.36
  263.1 0.1 copy.37
  263.2 0.1 copy.41
  263.3 0.1 copy.42
  263.4 0.1 copy.44
  263.5 0.1 copy.45
  263.6 0.8 copy.49
  264.4 1.4 copy.25
  265.9 1.4 copy.26
  267.3 0.7 copy.27
  268.0 2.2 concatenate.119
  270.2 2.1 fusion
  (42 shorter events, 1.1 us)
Async XLA Ops:
  6.5 181.2 %copy-start = (bf16[384,3072]{1,0:T(8,128)(2,1)S(1)}, bf16[384,3072]{1,0:T(8,128)(2,1)}, u32[]{:S(2)}) copy-start(bf16[384,3072]{1,0:T(8,128)(2,1)} %param.17) | copy-start | bytes 7077892
  6.5 120.0 %all-gather.4.cloned.1.call-start = ((), (), s32[]{:S(2)}) async-start(), calls=%async_computation.1 | async-start | bytes 12976128 | tf_op jit(solution)/shard_map/all_gather | solution.py:144
  8.5 167.4 %all-gather.6.cloned.1.call-start = ((), (), s32[]{:S(2)}) async-start(), calls=%async_computation.3 | async-start | bytes 37748736 | tf_op jit(solution)/shard_map/all_gather | solution.py:145
  126.6 0.7 copy-start.5
  126.6 49.3 %copy-start.1 = (bf16[256,384]{1,0:T(8,128)(2,1)S(1)}, bf16[256,384]{1,0:T(8,128)(2,1)}, u32[]{:S(2)}) copy-start(bf16[256,384]{1,0:T(8,128)(2,1)} %q_ref.1) | copy-start | bytes 589828
  126.6 104.1 %reduce-scatter.2.cloned.1.call-start = ((), (), s32[]{:S(2)}) async-start(), calls=%async_computation.2 | async-start | bytes 1966080 | tf_op jit(solution)/shard_map/reduce_scatter | solution.py:151
  187.7 2.2 copy-start.4
  187.7 43.0 %copy-start.2 = (bf16[64,3072]{1,0:T(8,128)(2,1)S(1)}, bf16[64,3072]{1,0:T(8,128)(2,1)}, u32[]{:S(2)}) copy-start(bf16[64,3072]{1,0:T(8,128)(2,1)} %param.16) | copy-start | bytes 1179652
  187.7 43.0 %copy-start.3 = (f32[3072]{0:T(1024)S(1)}, f32[3072]{0:T(1024)}, u32[]{:S(2)}) copy-start(f32[3072]{0:T(1024)} %param.18) | copy-start | bytes 36868
  189.9 43.4 %copy-start.6 = (bf16[3072,64]{0,1:T(8,128)(2,1)S(1)}, bf16[3072,64]{0,1:T(8,128)(2,1)}, u32[]{:S(2)}) copy-start(bf16[3072,64]{0,1:T(8,128)(2,1)} %param.21) | copy-start | bytes 1179652
  189.9 43.4 %copy-start.7 = (f32[3072]{0:T(1024)S(1)}, f32[3072]{0:T(1024)}, u32[]{:S(2)}) copy-start(f32[3072]{0:T(1024)} %param.19) | copy-start | bytes 36868
  235.1 7.3 %collective-permute-start = (bf16[1,1024]{1,0:T(2,128)(2,1)S(1)}, bf16[1,1024]{1,0:T(2,128)(2,1)S(1)}, u32[]{:S(2)}, u32[]{:S(2)}) collective-permute-start(bf16[1,1024]{1,0:T(2,128)(2,1)S(1)} %get-tuple-element.33), channel_id=1, source_target_pairs={{0,1},{1,2},{2,3},{3,4},{4,5},{5,6},{6,7},{7,8},{8,9},{9,10},{10,1... | collective-permute-start | bytes 6152 | tf_op jit(solution)/shard_map/ppermute | solution.py:27
  240.4 9.1 %collective-permute-start.1 = (bf16[1,1024]{1,0:T(2,128)(2,1)S(1)}, bf16[1,1024]{1,0:T(2,128)(2,1)S(1)}, u32[]{:S(2)}, u32[]{:S(2)}) collective-permute-start(bf16[1,1024]{1,0:T(2,128)(2,1)S(1)} %get-tuple-element.34), channel_id=1, source_target_pairs={{1,0},{2,1},{3,2},{4,3},{5,4},{6,5},{7,6},{8,7},{9,8},{10,9},{11,1... | collective-permute-start | bytes 6152 | tf_op jit(solution)/shard_map/ppermute | solution.py:29
  249.8 4.5 %collective-permute-start.2 = (bf16[6,1024]{1,0:T(8,128)(2,1)S(1)}, bf16[6,1024]{1,0:T(8,128)(2,1)S(1)}, u32[]{:S(2)}, u32[]{:S(2)}) collective-permute-start(bf16[6,1024]{1,0:T(8,128)(2,1)S(1)} %pad_maximum_fusion.3), channel_id=1, source_target_pairs={{0,32},{32,64},{64,96},{96,128},{128,160},{160,192},{192,224},{1,3... | collective-permute-start | bytes 36872 | tf_op jit(solution)/shard_map/ppermute | solution.py:39
  254.3 6.1 %collective-permute-start.3 = (bf16[6,1024]{1,0:T(8,128)(2,1)S(1)}, bf16[6,1024]{1,0:T(8,128)(2,1)S(1)}, u32[]{:S(2)}, u32[]{:S(2)}) collective-permute-start(bf16[6,1024]{1,0:T(8,128)(2,1)S(1)} %broadcast_select_fusion.1), channel_id=1, source_target_pairs={{0,32},{32,64},{64,96},{96,128},{128,160},{160,192},{192,224},{1,3... | collective-permute-start | bytes 36872 | tf_op jit(solution)/shard_map/ppermute | solution.py:39
Sparse Core Ops, SparseCore 0:
  9.9 116.6 all-gather.3
  128.4 47.4 all-gather.5
  190.0 40.6 reduce-scatter.1

commit v2 on v1

--- a/solution.py
+++ b/solution.py
@@ -141,19 +141,17 @@
     )
 
     kv = jnp.concatenate([key_vectors, values], axis=1)
-    kv = lax.all_gather(kv, ("z", "x"), axis=0, tiled=True)
-    kv = lax.all_gather(kv, "core", axis=0, tiled=False)
-    parts = kv.shape[0]
-    kv = kv.reshape(parts, FRAMES, kv.shape[1] // FRAMES, kv.shape[2])
+    kv = lax.all_gather(kv, ("z", "x", "core"), axis=0, tiled=True)
+    kv = kv.reshape(1, FRAMES, kv.shape[0] // FRAMES, kv.shape[1])
     attended = attend(scalars, queries, kv)
 
     tokens_dev = slab_rows // lax.axis_size(("head", "dec"))
-    projected = lax.psum_scatter(
-        jnp.dot(attended, out_weight, preferred_element_type=jnp.float32).astype(jnp.bfloat16),
-        ("head", "dec"),
-        scatter_dimension=0,
-        tiled=True,
-    ).astype(jnp.float32)
+    shares = lax.axis_size(("head", "dec"))
+    partial = jnp.dot(attended, out_weight, preferred_element_type=jnp.float32).astype(jnp.bfloat16)
+    partial = lax.all_to_all(
+        partial.reshape(shares, tokens_dev, partial.shape[1]), ("head", "dec"), 0, 0, tiled=False
+    )
+    projected = jnp.sum(partial.astype(jnp.float32), axis=0)
     hidden = residual.astype(jnp.float32) + branch_gate[None, :] * projected
     center = jnp.mean(hidden, axis=1, keepdims=True)
     spread = jnp.mean((hidden - center) ** 2, axis=1, keepdims=True)
@@ -170,11 +168,24 @@
         .transpose(0, 2, 1, 3, 4)
         .reshape(tile_rows, width * LC)
     )
-    padded = padded_2(tile, ((ROWS, 0),), 1)
-    prior_one = from_behind(padded, "z", 1)
-    prior_one = jnp.where(frame_index >= 1, prior_one, padded)
-    prior_two = from_behind(prior_one, "z", 1)
-    prior_two = jnp.where(frame_index >= 1, prior_two, padded)
+    per_frame = lax.axis_size(ROWS) // FRAMES
+    first_row = tile[:1]
+    last_row = tile[-1:]
+
+    def window_of(back):
+        shift = back * per_frame
+        return jnp.concatenate(
+            [
+                from_behind(last_row, ROWS, shift + 1),
+                tile if back == 0 else from_behind(tile, ROWS, shift),
+                from_behind(first_row, ROWS, shift - 1),
+            ],
+            axis=0,
+        )
+
+    padded = window_of(0)
+    prior_one = jnp.where(frame_index >= 1, window_of(1), padded)
+    prior_two = jnp.where(frame_index >= 2, window_of(2), prior_one)
     history = jnp.stack([prior_two, prior_one, padded]).reshape(3, tile_rows + 2, width, LC)
     history = jnp.pad(history, ((0, 0), (0, 0), (1, 1), (0, 0)))
     windows = [

time: 282 us -> 253 us (0.90)
  waiting for transfers between devices: 214 us -> 143 us
  starting transfers between devices: 15.6 us -> 50.7 us
  local copies, waits for them, and re-layouts: 12.3 us -> 20.4 us
    all_gather x2 -> x1, waiting for transfers between devices: 165 us -> 119 us  [per_device(): kv = lax.all_gather(kv, ('z', 'x', 'core'), axis=0, tiled=True)]
    reduce_scatter x1 -> x0, waiting for transfers between devices: 40.8 us -> none  [per_device(): lax.psum_scatter(jnp.dot(attended, out_weight, preferred_element_type=jnp...]
    ppermute x2 -> x8, starting transfers between devices: 8.28 us -> 44.7 us  [from_behind(): return lax.ppermute(x, axis, pairs)]
    all_to_all x0 -> x1, waiting for transfers between devices: none -> 18.9 us  [per_device(): lax.all_to_all(partial.reshape(shares, tokens_dev, partial.shape[1]), ('h...]
    ppermute x2 -> x0, starting transfers between devices: 7.21 us -> none  [the longest x1 5.29 us: padded_2(): lax.ppermute(tail, axis, [(i, (i + 1) % count) for i in range(ends)])]
    slice x23 -> x28, local copies, waits for them, and re-layouts: 8.21 us -> 15.4 us  [per_device(): history[time_tap, row_tap:row_tap + tile_rows, column_tap:column_tap + wi...]
    ppermute x2 -> x0, waiting for transfers between devices: 6.94 us -> none  [the longest x1 6.94 us: padded_2(): lax.ppermute(head, axis, [((i + 1) % count, i) for i in range(ends)])]
    all_to_all x0 -> x1, starting transfers between devices: none -> 5.98 us  [per_device(): lax.all_to_all(partial.reshape(shares, tokens_dev, partial.shape[1]), ('h...]
  transfers between devices with their start and end apart: 7 -> 10, of which waited for: 5 -> 3; matrix products, arithmetic and copies ran while one was open for 1% -> 1% of each run, Pallas kernels for 0% -> 0%
where the time goes in v2:
time: 253 us; the launch traced here: 249 us
  waiting for transfers between devices  143 us (57%)
  starting transfers between devices  50.7 us (20%)
  local copies, waits for them, and re-layouts  20.4 us (8%)
  between operations  14.3 us (6%)
  Pallas kernels  9.81 us (4%)
  other arithmetic  6.03 us (2%)
  matrix products  4.62 us (2%)
    all_gather x1, waiting for transfers between devices, per_device(): kv = lax.all_gather(kv, ('z', 'x', 'core'), axis=0, tiled=True)  119 us
    ppermute x8, starting transfers between devices, from_behind(): return lax.ppermute(x, axis, pairs)  44.7 us
    all_to_all x1, waiting for transfers between devices, per_device(): lax.all_to_all(partial.reshape(shares, tokens_dev, partial.shape[1]), ('h...  18.9 us
    slice x28, local copies, waits for them, and re-layouts, per_device(): history[time_tap, row_tap:row_tap + tile_rows, column_tap:column_tap + wi...  15.4 us
    pallas_call x1, Pallas kernels, attend(): pl.pallas_call(functools.partial(attend_kernel, head_count, part_rows), o...  9.81 us
    all_to_all x1, starting transfers between devices, per_device(): lax.all_to_all(partial.reshape(shares, tokens_dev, partial.shape[1]), ('h...  5.98 us
    ppermute x8, waiting for transfers between devices, from_behind(): return lax.ppermute(x, axis, pairs)  5.52 us
  transfers between devices with their start and end apart: 10, of which 3 were waited for; matrix products, arithmetic and copies ran while one was open for 1% of the time, Pallas kernels for 0%

profile of v2, /device:TPU:63, one launch (start us, length us, event | category | flops | bytes accessed | tf_op | source)
XLA Modules:
  0.0 249.0 jit_solution(3768820178460778857)
XLA Ops:
  6.5 2.0 pad_maximum_fusion
  8.6 1.4 fusion.11
  10.7 118.8 %all-gather.2.cloned.1.call-done = bf16[16384,768]{1,0:T(8,128)(2,1)} async-done(((bf16[256,768]{1,0:T(8,128)(2,1)}), bf16[16384,768]{1,0:T(8,128)(2,1)}) %all-gather.2.cloned.1.call-update) | async-done | bytes 25165840 | tf_op jit(solution)/shard_map/all_gather | solution.py:144
  129.4 0.9 copy-done.1
  130.3 9.8 %shard_map.118 = bf16[256,384]{1,0:T(8,128)(2,1)S(1)} custom-call(s32[5]{0:T(128)S(1)} %pad_add_fusion.sp_ref, bf16[256,384]{1,0:T(8,128)(2,1)S(1)} %copy-done.1, bf16[1,8,2048,768]{3,2,1,0:T(8,128)(2,1)} %bitcast.41), custom_call_target="tpu_custom_call" | custom-call | flops 4831838208 | bytes 19267584 | tf_op jit(solution)/shard_map/pallas_call | solution.py:90
  140.2 2.1 convolution_convert_fusion
  142.3 6.0 %all-to-all-start = ((bf16[4,64,3072]{2,1,0:T(8,128)(2,1)}), bf16[4,64,3072]{2,1,0:T(8,128)(2,1)}, u32[]{:S(2)}, u32[]{:S(2)}) async-start(bf16[4,64,3072]{2,1,0:T(8,128)(2,1)} %bitcast.42), calls=%async_computation | async-start | bytes 3145728 | tf_op jit(solution)/shard_map/all_to_all | solution.py:151
  148.3 18.9 %all-to-all-done = bf16[4,64,3072]{2,1,0:T(8,128)(2,1)} async-done(((bf16[4,64,3072]{2,1,0:T(8,128)(2,1)}), bf16[4,64,3072]{2,1,0:T(8,128)(2,1)}, u32[]{:S(2)}, u32[]{:S(2)}) %all-to-all-start) | async-done | bytes 1572896 | tf_op jit(solution)/shard_map/all_to_all | solution.py:151
  167.2 1.7 convert_reduce_fusion
  168.9 0.2 fusion.5
  169.2 0.3 multiply_reduce_fusion
  169.5 0.4 convolution_convert_fusion.1
  170.1 0.1 copy.18
  170.2 0.1 reshape.297
  170.4 10.2 %collective-permute-start.6 = (bf16[1,1024]{1,0:T(2,128)(2,1)S(1)}, bf16[1,1024]{1,0:T(2,128)(2,1)S(1)}, u32[]{:S(2)}, u32[]{:S(2)}) collective-permute-start(bf16[1,1024]{1,0:T(2,128)(2,1)S(1)} %get-tuple-element.35), channel_id=1, source_target_pairs={{0,1},{1,2},{2,3},{3,4},{4,5},{5,6},{6,7},{7,8},{8,9},{9,10},{10,1... | collective-permute-start | bytes 6152 | tf_op jit(solution)/shard_map/ppermute | solution.py:39
  180.5 1.9 collective-permute-start.7
  182.5 16.7 %collective-permute-start = (bf16[1,1024]{1,0:T(2,128)(2,1)S(1)}, bf16[1,1024]{1,0:T(2,128)(2,1)S(1)}, u32[]{:S(2)}, u32[]{:S(2)}) collective-permute-start(bf16[1,1024]{1,0:T(2,128)(2,1)S(1)} %get-tuple-element.35), channel_id=1, source_target_pairs={{0,65},{1,66},{2,67},{3,68},{4,69},{5,70},{6,71},{7,72},{8,73},{9,... | collective-permute-start | bytes 6152 | tf_op jit(solution)/shard_map/ppermute | solution.py:39
  199.2 3.3 %collective-permute-start.1 = (bf16[4,1024]{1,0:T(4,128)(2,1)S(1)}, bf16[4,1024]{1,0:T(4,128)(2,1)S(1)}, u32[]{:S(2)}, u32[]{:S(2)}) collective-permute-start(bf16[4,1024]{1,0:T(4,128)(2,1)S(1)} %reshape.297), channel_id=1, source_target_pairs={{0,64},{1,65},{2,66},{3,67},{4,68},{5,69},{6,70},{7,71},{8,72},{9,... | collective-permute-start | bytes 24584 | tf_op jit(solution)/shard_map/ppermute | solution.py:39
  202.5 2.3 collective-permute-start.4
  204.9 1.9 collective-permute-start.2
  207.1 6.4 %collective-permute-start.3 = (bf16[1,1024]{1,0:T(2,128)(2,1)S(1)}, bf16[1,1024]{1,0:T(2,128)(2,1)S(1)}, u32[]{:S(2)}, u32[]{:S(2)}) collective-permute-start(bf16[1,1024]{1,0:T(2,128)(2,1)S(1)} %get-tuple-element.35), channel_id=1, source_target_pairs={{0,33},{1,34},{2,35},{3,36},{4,37},{5,38},{6,39},{7,40},{8,41},{9,... | collective-permute-start | bytes 6152 | tf_op jit(solution)/shard_map/ppermute | solution.py:39
  213.7 1.9 collective-permute-start.5
  215.6 0.1 copy.50
  216.4 5.5 %collective-permute-done.5 = bf16[1,1024]{1,0:T(2,128)(2,1)S(1)} collective-permute-done((bf16[1,1024]{1,0:T(2,128)(2,1)S(1)}, bf16[1,1024]{1,0:T(2,128)(2,1)S(1)}, u32[]{:S(2)}, u32[]{:S(2)}) %collective-permute-start.5) | collective-permute-done | bytes 2080 | tf_op jit(solution)/shard_map/ppermute | solution.py:39
  222.1 0.1 concatenate.136
  222.3 0.1 concatenate.140
  222.7 0.1 copy.33
  222.9 0.1 copy.39
  223.0 0.1 copy.42
  223.1 0.1 copy.45
  223.2 0.1 copy.30
  223.3 0.7 fusion.12
  224.3 0.1 copy.37
  224.4 0.1 copy.38
  224.6 0.1 copy.41
  224.7 0.1 copy.43
  224.9 0.8 copy.46
  225.8 1.4 copy.47
  227.2 1.4 copy.51
  228.6 1.4 copy.52
  230.0 1.4 copy.54
  231.5 1.4 copy.55
  232.9 1.4 copy.59
  234.3 1.4 copy.29
  235.7 1.4 copy.31
  237.2 0.7 copy.32
  237.9 2.2 concatenate.176
  240.1 2.1 fusion
  (60 shorter events, 2.5 us)
Async XLA Ops:
  6.5 133.6 %copy-start = (bf16[384,3072]{1,0:T(8,128)(2,1)S(1)}, bf16[384,3072]{1,0:T(8,128)(2,1)}, u32[]{:S(2)}) copy-start(bf16[384,3072]{1,0:T(8,128)(2,1)} %param.17) | copy-start | bytes 7077892
  6.5 122.9 %all-gather.2.cloned.1.call-start = ((), (), s32[]{:S(2)}) async-start(), calls=%async_computation.1 | async-start | bytes 25559040 | tf_op jit(solution)/shard_map/all_gather | solution.py:144
  129.4 0.9 copy-start.1
  142.3 6.0 %copy-start.4 = (f32[3072]{0:T(1024)S(1)}, f32[3072]{0:T(1024)}, u32[]{:S(2)}) copy-start(f32[3072]{0:T(1024)} %param.20) | copy-start | bytes 36868
  142.3 26.6 %copy-start.2 = (bf16[64,3072]{1,0:T(8,128)(2,1)S(1)}, bf16[64,3072]{1,0:T(8,128)(2,1)}, u32[]{:S(2)}) copy-start(bf16[64,3072]{1,0:T(8,128)(2,1)} %param.16) | copy-start | bytes 1179652
  142.3 26.6 %copy-start.3 = (f32[3072]{0:T(1024)S(1)}, f32[3072]{0:T(1024)}, u32[]{:S(2)}) copy-start(f32[3072]{0:T(1024)} %param.18) | copy-start | bytes 36868
  142.3 24.9 %all-to-all-start = ((bf16[4,64,3072]{2,1,0:T(8,128)(2,1)}), bf16[4,64,3072]{2,1,0:T(8,128)(2,1)}, u32[]{:S(2)}, u32[]{:S(2)}) async-start(bf16[4,64,3072]{2,1,0:T(8,128)(2,1)} %bitcast.42), calls=%async_computation | async-start | bytes 3145728 | tf_op jit(solution)/shard_map/all_to_all | solution.py:151
  148.3 21.2 %copy-start.5 = (bf16[3072,64]{0,1:T(8,128)(2,1)S(1)}, bf16[3072,64]{0,1:T(8,128)(2,1)}, u32[]{:S(2)}) copy-start(bf16[3072,64]{0,1:T(8,128)(2,1)} %param.21) | copy-start | bytes 1179652
  148.3 21.2 %copy-start.6 = (f32[3072]{0:T(1024)S(1)}, f32[3072]{0:T(1024)}, u32[]{:S(2)}) copy-start(f32[3072]{0:T(1024)} %param.19) | copy-start | bytes 36868
  170.4 34.6 %collective-permute-start.6 = (bf16[1,1024]{1,0:T(2,128)(2,1)S(1)}, bf16[1,1024]{1,0:T(2,128)(2,1)S(1)}, u32[]{:S(2)}, u32[]{:S(2)}) collective-permute-start(bf16[1,1024]{1,0:T(2,128)(2,1)S(1)} %get-tuple-element.35), channel_id=1, source_target_pairs={{0,1},{1,2},{2,3},{3,4},{4,5},{5,6},{6,7},{7,8},{8,9},{9,10},{10,1... | collective-permute-start | bytes 6152 | tf_op jit(solution)/shard_map/ppermute | solution.py:39
  180.5 26.5 %collective-permute-start.7 = (bf16[1,1024]{1,0:T(2,128)(2,1)S(1)}, bf16[1,1024]{1,0:T(2,128)(2,1)S(1)}, u32[]{:S(2)}, u32[]{:S(2)}) collective-permute-start(bf16[1,1024]{1,0:T(2,128)(2,1)S(1)} %get-tuple-element.36), channel_id=1, source_target_pairs={{1,0},{2,1},{3,2},{4,3},{5,4},{6,5},{7,6},{8,7},{9,8},{10,9},{11,1... | collective-permute-start | bytes 6152 | tf_op jit(solution)/shard_map/ppermute | solution.py:39
  182.5 31.2 %collective-permute-start = (bf16[1,1024]{1,0:T(2,128)(2,1)S(1)}, bf16[1,1024]{1,0:T(2,128)(2,1)S(1)}, u32[]{:S(2)}, u32[]{:S(2)}) collective-permute-start(bf16[1,1024]{1,0:T(2,128)(2,1)S(1)} %get-tuple-element.35), channel_id=1, source_target_pairs={{0,65},{1,66},{2,67},{3,68},{4,69},{5,70},{6,71},{7,72},{8,73},{9,... | collective-permute-start | bytes 6152 | tf_op jit(solution)/shard_map/ppermute | solution.py:39
  199.2 22.9 %collective-permute-start.1 = (bf16[4,1024]{1,0:T(4,128)(2,1)S(1)}, bf16[4,1024]{1,0:T(4,128)(2,1)S(1)}, u32[]{:S(2)}, u32[]{:S(2)}) collective-permute-start(bf16[4,1024]{1,0:T(4,128)(2,1)S(1)} %reshape.297), channel_id=1, source_target_pairs={{0,64},{1,65},{2,66},{3,67},{4,68},{5,69},{6,70},{7,71},{8,72},{9,... | collective-permute-start | bytes 24584 | tf_op jit(solution)/shard_map/ppermute | solution.py:39
  202.5 19.8 %collective-permute-start.4 = (bf16[4,1024]{1,0:T(4,128)(2,1)S(1)}, bf16[4,1024]{1,0:T(4,128)(2,1)S(1)}, u32[]{:S(2)}, u32[]{:S(2)}) collective-permute-start(bf16[4,1024]{1,0:T(4,128)(2,1)S(1)} %reshape.297), channel_id=1, source_target_pairs={{0,32},{1,33},{2,34},{3,35},{4,36},{5,37},{6,38},{7,39},{8,40},{9,... | collective-permute-start | bytes 24584 | tf_op jit(solution)/shard_map/ppermute | solution.py:39
  204.9 11.1 %collective-permute-start.2 = (bf16[1,1024]{1,0:T(2,128)(2,1)S(1)}, bf16[1,1024]{1,0:T(2,128)(2,1)S(1)}, u32[]{:S(2)}, u32[]{:S(2)}) collective-permute-start(bf16[1,1024]{1,0:T(2,128)(2,1)S(1)} %get-tuple-element.36), channel_id=1, source_target_pairs={{0,63},{1,64},{2,65},{3,66},{4,67},{5,68},{6,69},{7,70},{8,71},{9,... | collective-permute-start | bytes 6152 | tf_op jit(solution)/shard_map/ppermute | solution.py:39
  207.1 9.2 %collective-permute-start.3 = (bf16[1,1024]{1,0:T(2,128)(2,1)S(1)}, bf16[1,1024]{1,0:T(2,128)(2,1)S(1)}, u32[]{:S(2)}, u32[]{:S(2)}) collective-permute-start(bf16[1,1024]{1,0:T(2,128)(2,1)S(1)} %get-tuple-element.35), channel_id=1, source_target_pairs={{0,33},{1,34},{2,35},{3,36},{4,37},{5,38},{6,39},{7,40},{8,41},{9,... | collective-permute-start | bytes 6152 | tf_op jit(solution)/shard_map/ppermute | solution.py:39
  213.7 8.3 %collective-permute-start.5 = (bf16[1,1024]{1,0:T(2,128)(2,1)S(1)}, bf16[1,1024]{1,0:T(2,128)(2,1)S(1)}, u32[]{:S(2)}, u32[]{:S(2)}) collective-permute-start(bf16[1,1024]{1,0:T(2,128)(2,1)S(1)} %get-tuple-element.36), channel_id=1, source_target_pairs={{0,31},{1,32},{2,33},{3,34},{4,35},{5,36},{6,37},{7,38},{8,39},{9,... | collective-permute-start | bytes 6152 | tf_op jit(solution)/shard_map/ppermute | solution.py:39
Sparse Core Ops, SparseCore 0:
  10.1 119.2 all-gather.1

commit v3 on v2

--- a/solution.py
+++ b/solution.py
@@ -16,23 +16,6 @@
 ROWS = ("z", "x", "core", "head", "dec")
 
 
-def padded_2(cells, sides, width):
-    for axis, dim in sides:
-        count = lax.axis_size(axis)
-        ends = count - 1
-        head = lax.slice_in_dim(cells, 0, width, axis=dim)
-        tail = lax.slice_in_dim(cells, cells.shape[dim] - width, cells.shape[dim], axis=dim)
-        cells = jnp.concatenate(
-            [
-                lax.ppermute(tail, axis, [(i, (i + 1) % count) for i in range(ends)]),
-                cells,
-                lax.ppermute(head, axis, [((i + 1) % count, i) for i in range(ends)]),
-            ],
-            axis=dim,
-        )
-    return cells
-
-
 def from_behind(x, axis, by):
     peers = lax.axis_size(axis)
     pairs = [(i, i + by) for i in range(peers) if 0 <= i + by < peers]
@@ -52,6 +35,8 @@
         l_sc[...] = jnp.zeros(l_sc.shape, jnp.float32)
         acc_sc[...] = jnp.zeros(acc_sc.shape, jnp.float32)
 
+    to_log2 = DH ** (-0.5) * 1.4426950408889634
+    ones = jnp.ones((kv_ref.shape[1], DH), jnp.bfloat16)
     for h in range(head_count):
         seen = (frame <= frame_now) & (frame >= frame_now - sp_ref[2 + h])
 
@@ -63,12 +48,13 @@
                 v = kv_ref[c, :, hd + h * DH:hd + (h + 1) * DH]
                 s = lax.dot_general(
                     q, k, (((1,), (1,)), ((), ())), preferred_element_type=jnp.float32
-                ) * DH ** (-0.5)
+                ) * to_log2
                 m_old = m_sc[h]
                 m_new = jnp.maximum(m_old, jnp.max(s, axis=1, keepdims=True))
-                alpha = jnp.exp(m_old - m_new)
-                p = jnp.exp(s - m_new).astype(jnp.bfloat16)
-                l_sc[h] = alpha * l_sc[h] + jnp.sum(p.astype(jnp.float32), axis=1, keepdims=True)
+                alpha = jnp.exp2(m_old - m_new)
+                p = jnp.exp2(s - m_new).astype(jnp.bfloat16)
+                total = jnp.dot(p, ones, preferred_element_type=jnp.float32)[:, :1]
+                l_sc[h] = alpha * l_sc[h] + total
                 acc_sc[h] = alpha * acc_sc[h] + jnp.dot(p, v, preferred_element_type=jnp.float32)
                 m_sc[h] = m_new
 
@@ -147,11 +133,15 @@
 
     tokens_dev = slab_rows // lax.axis_size(("head", "dec"))
     shares = lax.axis_size(("head", "dec"))
-    partial = jnp.dot(attended, out_weight, preferred_element_type=jnp.float32).astype(jnp.bfloat16)
-    partial = lax.all_to_all(
-        partial.reshape(shares, tokens_dev, partial.shape[1]), ("head", "dec"), 0, 0, tiled=False
-    )
-    projected = jnp.sum(partial.astype(jnp.float32), axis=0)
+    weight_all = lax.all_to_all(
+        jnp.broadcast_to(out_weight[None], (shares,) + out_weight.shape),
+        ("head", "dec"), 0, 0, tiled=False,
+    ).reshape(shares * out_weight.shape[0], out_weight.shape[1])
+    mine = lax.all_to_all(
+        attended.reshape(shares, tokens_dev, attended.shape[1]), ("head", "dec"), 0, 0, tiled=False
+    )
+    mine = mine.transpose(1, 0, 2).reshape(tokens_dev, shares * attended.shape[1])
+    projected = jnp.dot(mine, weight_all, preferred_element_type=jnp.float32)
     hidden = residual.astype(jnp.float32) + branch_gate[None, :] * projected
     center = jnp.mean(hidden, axis=1, keepdims=True)
     spread = jnp.mean((hidden - center) ** 2, axis=1, keepdims=True)
@@ -172,20 +162,11 @@
     first_row = tile[:1]
     last_row = tile[-1:]
 
-    def window_of(back):
-        shift = back * per_frame
-        return jnp.concatenate(
-            [
-                from_behind(last_row, ROWS, shift + 1),
-                tile if back == 0 else from_behind(tile, ROWS, shift),
-                from_behind(first_row, ROWS, shift - 1),
-            ],
-            axis=0,
-        )
-
-    padded = window_of(0)
-    prior_one = jnp.where(frame_index >= 1, window_of(1), padded)
-    prior_two = jnp.where(frame_index >= 2, window_of(2), prior_one)
+    padded = jnp.concatenate(
+        [from_behind(last_row, ROWS, 1), tile, from_behind(first_row, ROWS, -1)], axis=0
+    )
+    prior_one = jnp.where(frame_index >= 1, from_behind(padded, ROWS, per_frame), padded)
+    prior_two = jnp.where(frame_index >= 2, from_behind(padded, ROWS, 2 * per_frame), prior_one)
     history = jnp.stack([prior_two, prior_one, padded]).reshape(3, tile_rows + 2, width, LC)
     history = jnp.pad(history, ((0, 0), (0, 0), (1, 1), (0, 0)))
     windows = [

time: 253 us -> 202 us (0.80)
  waiting for transfers between devices: 143 us -> 118 us
  starting transfers between devices: 50.7 us -> 35.6 us
  local copies, waits for them, and re-layouts: 20.4 us -> 10.9 us
  other arithmetic: 6.03 us -> 3.13 us
    ppermute x8 -> x4, starting transfers between devices: 44.7 us -> 24.6 us  [from_behind(): return lax.ppermute(x, axis, pairs)]
    all_to_all x1 -> x2, waiting for transfers between devices: 18.9 us -> 3.71 us  [the longest x1 3.71 us: per_device(): lax.all_to_all(attended.reshape(shares, tokens_dev, attended.shape[1]), (...]
    slice x28 -> x23, local copies, waits for them, and re-layouts: 15.4 us -> 2.3 us  [per_device(): history[time_tap, row_tap:row_tap + tile_rows, column_tap:column_tap + wi...]
    all_gather x1, waiting for transfers between devices: 119 us -> 107 us  [per_device(): kv = lax.all_gather(kv, ('z', 'x', 'core'), axis=0, tiled=True)]
    broadcast_in_dim x0 -> x1, local copies, waits for them, and re-layouts: none -> 6.52 us  [per_device(): jnp.broadcast_to(out_weight[None], (shares,) + out_weight.shape)]
    all_to_all x1 -> x2, starting transfers between devices: 5.98 us -> 11 us  [the longest x1 5.91 us: per_device(): lax.all_to_all(jnp.broadcast_to(out_weight[None], (shares,) + out_weight....]
    dot_general x1, matrix products: 2.13 us -> 5.57 us  [per_device(): projected = jnp.dot(mine, weight_all, preferred_element_type=jnp.float32)]
    ppermute x8 -> x4, waiting for transfers between devices: 5.52 us -> 7.61 us  [from_behind(): return lax.ppermute(x, axis, pairs)]
  transfers between devices with their start and end apart: 10 -> 7, of which waited for: 3 -> 4; matrix products, arithmetic and copies ran while one was open for 1% -> 4% of each run, Pallas kernels for 0% -> 5%
where the time goes in v3:
time: 202 us; the launch traced here: 200 us
  waiting for transfers between devices  118 us (58%)
  starting transfers between devices  35.6 us (18%)
  between operations  14.3 us (7%)
  local copies, waits for them, and re-layouts  10.9 us (5%)
  Pallas kernels  10.5 us (5%)
  matrix products  6.92 us (3%)
  other arithmetic  3.13 us (2%)
    all_gather x1, waiting for transfers between devices, per_device(): kv = lax.all_gather(kv, ('z', 'x', 'core'), axis=0, tiled=True)  107 us
    ppermute x4, starting transfers between devices, from_behind(): return lax.ppermute(x, axis, pairs)  24.6 us
    pallas_call x1, Pallas kernels, attend(): pl.pallas_call(functools.partial(attend_kernel, head_count, part_rows), o...  10.5 us
    ppermute x4, waiting for transfers between devices, from_behind(): return lax.ppermute(x, axis, pairs)  7.61 us
    broadcast_in_dim x1, local copies, waits for them, and re-layouts, per_device(): jnp.broadcast_to(out_weight[None], (shares,) + out_weight.shape)  6.52 us
    all_to_all x1, starting transfers between devices, per_device(): lax.all_to_all(jnp.broadcast_to(out_weight[None], (shares,) + out_weight....  5.91 us
    dot_general x1, matrix products, per_device(): projected = jnp.dot(mine, weight_all, preferred_element_type=jnp.float32)  5.57 us
    all_to_all x1, starting transfers between devices, per_device(): lax.all_to_all(attended.reshape(shares, tokens_dev, attended.shape[1]), (...  5.05 us
  transfers between devices with their start and end apart: 7, of which 4 were waited for; matrix products, arithmetic and copies ran while one was open for 4% of the time, Pallas kernels for 5%

profile of v3, /device:TPU:63, one launch (start us, length us, event | category | flops | bytes accessed | tf_op | source)
XLA Modules:
  0.0 199.8 jit_solution(18352432869986146492)
XLA Ops:
  6.5 1.8 pad_maximum_fusion
  8.4 6.5 %broadcast_in_dim.2 = bf16[4,384,3072]{2,1,0:T(8,128)(2,1)} broadcast(bf16[384,3072]{1,0:T(8,128)(2,1)} %param.17), dimensions={1,2} | broadcast | bytes 11796480 | tf_op jit(solution)/shard_map/broadcast_in_dim | solution.py:137
  14.9 5.9 %all-to-all-start.1 = ((bf16[4,384,3072]{2,1,0:T(8,128)(2,1)}), bf16[4,384,3072]{2,1,0:T(8,128)(2,1)}, u32[]{:S(2)}, u32[]{:S(2)}) async-start(bf16[4,384,3072]{2,1,0:T(8,128)(2,1)} %broadcast_in_dim.2), calls=%async_computation.1 | async-start | bytes 18874368 | tf_op jit(solution)/shard_map/all_to_all | solution.py:136
  20.9 0.7 fusion.13
  22.3 107.1 %all-gather.2.cloned.1.call-done = bf16[16384,768]{1,0:T(8,128)(2,1)} async-done(((bf16[256,768]{1,0:T(8,128)(2,1)}), bf16[16384,768]{1,0:T(8,128)(2,1)}) %all-gather.2.cloned.1.call-update) | async-done | bytes 25165840 | tf_op jit(solution)/shard_map/all_gather | solution.py:130
  129.4 10.5 %shard_map.118 = bf16[256,384]{1,0:T(8,128)(2,1)} custom-call(s32[5]{0:T(128)S(1)} %pad_add_fusion.sp_ref, bf16[256,384]{1,0:T(8,128)(2,1)S(1)} %copy-done.1, bf16[1,8,2048,768]{3,2,1,0:T(8,128)(2,1)} %bitcast.51), custom_call_target="tpu_custom_call" | custom-call | flops 4831838208 | bytes 19267584 | tf_op jit(solution)/shard_map/pallas_call | solution.py:76
  139.9 5.0 %all-to-all-start = ((bf16[4,64,384]{2,1,0:T(8,128)(2,1)}), bf16[4,64,384]{2,1,0:T(8,128)(2,1)S(1)}, u32[]{:S(2)}, u32[]{:S(2)}) async-start(bf16[4,64,384]{2,1,0:T(8,128)(2,1)} %bitcast.3), calls=%async_computation | async-start | bytes 393216 | tf_op jit(solution)/shard_map/all_to_all | solution.py:140
  145.0 3.7 %all-to-all-done = bf16[4,64,384]{2,1,0:T(8,128)(2,1)S(1)} async-done(((bf16[4,64,384]{2,1,0:T(8,128)(2,1)}), bf16[4,64,384]{2,1,0:T(8,128)(2,1)S(1)}, u32[]{:S(2)}, u32[]{:S(2)}) %all-to-all-start) | async-done | bytes 196640 | tf_op jit(solution)/shard_map/all_to_all | solution.py:140
  148.7 5.6 %fusion.18 = (f32[64]{0:T(128)S(1)}, f32[64,3072]{1,0:T(8,128)S(1)}) fusion(bf16[4,384,3072]{2,1,0:T(8,128)(2,1)} %all-to-all-done.1, bf16[4,64,384]{2,1,0:T(8,128)(2,1)S(1)} %all-to-all-done, f32[3072]{0:T(1024)S(1)} %copy-done.3, bf16[64,3072]{1,0:T(8,128)(2,1)S(1)} %copy-done.2), kind=kOutput, calls=%fused_computation.37 | convolution fusion | flops 604766144 | bytes 10825984 | tf_op jit(solution)/shard_map/dot_general | solution.py:144
  154.3 0.3 multiply_reduce_fusion
  154.6 0.3 convolution_convert_fusion
  154.9 0.1 copy.17
  155.1 0.1 copy.18
  155.2 0.1 reshape.105
  155.4 10.5 %collective-permute-start = (bf16[1,1024]{1,0:T(2,128)(2,1)S(1)}, bf16[1,1024]{1,0:T(2,128)(2,1)S(1)}, u32[]{:S(2)}, u32[]{:S(2)}) collective-permute-start(bf16[1,1024]{1,0:T(2,128)(2,1)S(1)} %get-tuple-element.35), channel_id=1, source_target_pairs={{0,1},{1,2},{2,3},{3,4},{4,5},{5,6},{6,7},{7,8},{8,9},{9,10},{10,1... | collective-permute-start | bytes 6152 | tf_op jit(solution)/shard_map/ppermute | solution.py:22
  165.9 1.9 collective-permute-start.1
  167.9 7.1 %collective-permute-done.1 = bf16[1,1024]{1,0:T(2,128)(2,1)S(1)} collective-permute-done((bf16[1,1024]{1,0:T(2,128)(2,1)S(1)}, bf16[1,1024]{1,0:T(2,128)(2,1)S(1)}, u32[]{:S(2)}, u32[]{:S(2)}) %collective-permute-start.1) | collective-permute-done | bytes 2080 | tf_op jit(solution)/shard_map/ppermute | solution.py:22
  175.0 8.8 %collective-permute-start.2 = (bf16[6,1024]{1,0:T(8,128)(2,1)S(1)}, bf16[6,1024]{1,0:T(8,128)(2,1)S(1)}, u32[]{:S(2)}, u32[]{:S(2)}) collective-permute-start(bf16[6,1024]{1,0:T(8,128)(2,1)S(1)} %pad_maximum_fusion.3), channel_id=1, source_target_pairs={{0,64},{1,65},{2,66},{3,67},{4,68},{5,69},{6,70},{7,71},{8,72},{9,... | collective-permute-start | bytes 36872 | tf_op jit(solution)/shard_map/ppermute | solution.py:22
  183.9 3.3 %collective-permute-start.3 = (bf16[6,1024]{1,0:T(8,128)(2,1)S(1)}, bf16[6,1024]{1,0:T(8,128)(2,1)S(1)}, u32[]{:S(2)}, u32[]{:S(2)}) collective-permute-start(bf16[6,1024]{1,0:T(8,128)(2,1)S(1)} %pad_maximum_fusion.3), channel_id=1, source_target_pairs={{0,32},{1,33},{2,34},{3,35},{4,36},{5,37},{6,38},{7,39},{8,40},{9,... | collective-permute-start | bytes 36872 | tf_op jit(solution)/shard_map/ppermute | solution.py:22
  187.7 0.1 copy.40
  187.8 0.1 copy.48
  187.9 0.5 collective-permute-done.3
  188.4 0.1 stack.18
  188.5 0.1 copy.23
  188.7 0.1 stack.19
  188.8 0.1 copy.24
  188.9 0.1 fusion.9
  189.0 0.1 fusion.16
  189.2 0.1 copy.26
  189.3 0.1 copy.27
  189.4 0.1 copy.28
  189.5 0.1 copy.29
  189.6 0.1 copy.30
  189.7 0.1 copy.31
  189.8 0.1 copy.32
  189.9 0.1 copy.33
  190.0 0.1 copy.34
  190.1 0.1 copy.35
  190.2 0.1 copy.36
  190.3 0.1 copy.37
  190.5 0.1 copy.41
  190.6 0.1 copy.42
  190.7 0.1 copy.44
  190.8 0.1 copy.45
  190.9 0.1 copy.49
  191.0 0.1 copy.25
  191.1 0.8 concatenate.119
  192.0 1.0 fusion.2
  (41 shorter events, 0.9 us)
Async XLA Ops:
  6.5 185.4 %copy-start = (bf16[432,512]{1,0:T(8,128)(2,1)S(1)}, bf16[432,512]{1,0:T(8,128)(2,1)}, u32[]{:S(2)}) copy-start(bf16[432,512]{1,0:T(8,128)(2,1)} %param.22) | copy-start | bytes 1327108
  6.5 122.9 %all-gather.2.cloned.1.call-start = ((), (), s32[]{:S(2)}) async-start(), calls=%async_computation.2 | async-start | bytes 25559040 | tf_op jit(solution)/shard_map/all_gather | solution.py:130
  14.9 5.9 %copy-start.5 = (s32[12]{0:T(128)S(1)}, s32[12]{0:T(128)}, u32[]{:S(2)}) copy-start(s32[12]{0:T(128)} %param.15) | copy-start | bytes 148
  14.9 114.5 %copy-start.1 = (bf16[256,384]{1,0:T(8,128)(2,1)S(1)}, bf16[256,384]{1,0:T(8,128)(2,1)}, u32[]{:S(2)}) copy-start(bf16[256,384]{1,0:T(8,128)(2,1)} %q_ref.1) | copy-start | bytes 589828
  14.9 125.0 %all-to-all-start.1 = ((bf16[4,384,3072]{2,1,0:T(8,128)(2,1)}), bf16[4,384,3072]{2,1,0:T(8,128)(2,1)}, u32[]{:S(2)}, u32[]{:S(2)}) async-start(bf16[4,384,3072]{2,1,0:T(8,128)(2,1)} %broadcast_in_dim.2), calls=%async_computation.1 | async-start | bytes 18874368 | tf_op jit(solution)/shard_map/all_to_all | solution.py:136
  129.4 15.6 %copy-start.4 = (f32[3072]{0:T(1024)S(1)}, f32[3072]{0:T(1024)}, u32[]{:S(2)}) copy-start(f32[3072]{0:T(1024)} %param.20) | copy-start | bytes 36868
  129.4 19.3 %copy-start.2 = (bf16[64,3072]{1,0:T(8,128)(2,1)S(1)}, bf16[64,3072]{1,0:T(8,128)(2,1)}, u32[]{:S(2)}) copy-start(bf16[64,3072]{1,0:T(8,128)(2,1)} %param.16) | copy-start | bytes 1179652
  129.4 19.3 %copy-start.3 = (f32[3072]{0:T(1024)S(1)}, f32[3072]{0:T(1024)}, u32[]{:S(2)}) copy-start(f32[3072]{0:T(1024)} %param.18) | copy-start | bytes 36868
  139.9 14.6 %copy-start.6 = (bf16[3072,64]{0,1:T(8,128)(2,1)S(1)}, bf16[3072,64]{0,1:T(8,128)(2,1)}, u32[]{:S(2)}) copy-start(bf16[3072,64]{0,1:T(8,128)(2,1)} %param.21) | copy-start | bytes 1179652
  139.9 14.6 %copy-start.7 = (f32[3072]{0:T(1024)S(1)}, f32[3072]{0:T(1024)}, u32[]{:S(2)}) copy-start(f32[3072]{0:T(1024)} %param.19) | copy-start | bytes 36868
  139.9 8.8 %all-to-all-start = ((bf16[4,64,384]{2,1,0:T(8,128)(2,1)}), bf16[4,64,384]{2,1,0:T(8,128)(2,1)S(1)}, u32[]{:S(2)}, u32[]{:S(2)}) async-start(bf16[4,64,384]{2,1,0:T(8,128)(2,1)} %bitcast.3), calls=%async_computation | async-start | bytes 393216 | tf_op jit(solution)/shard_map/all_to_all | solution.py:140
  145.0 47.0 %copy-start.8 = (f32[512]{0:T(512)S(1)}, f32[512]{0:T(512)}, u32[]{:S(2)}) copy-start(f32[512]{0:T(512)} %param.23) | copy-start | bytes 6148
  155.4 12.5 %collective-permute-start = (bf16[1,1024]{1,0:T(2,128)(2,1)S(1)}, bf16[1,1024]{1,0:T(2,128)(2,1)S(1)}, u32[]{:S(2)}, u32[]{:S(2)}) collective-permute-start(bf16[1,1024]{1,0:T(2,128)(2,1)S(1)} %get-tuple-element.35), channel_id=1, source_target_pairs={{0,1},{1,2},{2,3},{3,4},{4,5},{5,6},{6,7},{7,8},{8,9},{9,10},{10,1... | collective-permute-start | bytes 6152 | tf_op jit(solution)/shard_map/ppermute | solution.py:22
  165.9 9.1 %collective-permute-start.1 = (bf16[1,1024]{1,0:T(2,128)(2,1)S(1)}, bf16[1,1024]{1,0:T(2,128)(2,1)S(1)}, u32[]{:S(2)}, u32[]{:S(2)}) collective-permute-start(bf16[1,1024]{1,0:T(2,128)(2,1)S(1)} %get-tuple-element.36), channel_id=1, source_target_pairs={{1,0},{2,1},{3,2},{4,3},{5,4},{6,5},{7,6},{8,7},{9,8},{10,9},{11,1... | collective-permute-start | bytes 6152 | tf_op jit(solution)/shard_map/ppermute | solution.py:22
  175.0 12.8 %collective-permute-start.2 = (bf16[6,1024]{1,0:T(8,128)(2,1)S(1)}, bf16[6,1024]{1,0:T(8,128)(2,1)S(1)}, u32[]{:S(2)}, u32[]{:S(2)}) collective-permute-start(bf16[6,1024]{1,0:T(8,128)(2,1)S(1)} %pad_maximum_fusion.3), channel_id=1, source_target_pairs={{0,64},{1,65},{2,66},{3,67},{4,68},{5,69},{6,70},{7,71},{8,72},{9,... | collective-permute-start | bytes 36872 | tf_op jit(solution)/shard_map/ppermute | solution.py:22
  183.9 4.5 %collective-permute-start.3 = (bf16[6,1024]{1,0:T(8,128)(2,1)S(1)}, bf16[6,1024]{1,0:T(8,128)(2,1)S(1)}, u32[]{:S(2)}, u32[]{:S(2)}) collective-permute-start(bf16[6,1024]{1,0:T(8,128)(2,1)S(1)} %pad_maximum_fusion.3), channel_id=1, source_target_pairs={{0,32},{1,33},{2,34},{3,35},{4,36},{5,37},{6,38},{7,39},{8,40},{9,... | collective-permute-start | bytes 36872 | tf_op jit(solution)/shard_map/ppermute | solution.py:22
Sparse Core Ops, SparseCore 0:
  10.1 119.2 all-gather.1

commit v4 on v3

--- a/solution.py
+++ b/solution.py
@@ -22,7 +22,7 @@
     return lax.ppermute(x, axis, pairs)
 
 
-def attend_kernel(head_count, part_rows, sp_ref, q_ref, kv_ref, o_ref, m_sc, l_sc, acc_sc):
+def attend_kernel(head_count, sp_ref, q_ref, kv_ref, o_ref, m_sc, l_sc, acc_sc):
     step = pl.program_id(0)
     frame_now = sp_ref[0]
     first = sp_ref[1]
@@ -36,7 +36,6 @@
         acc_sc[...] = jnp.zeros(acc_sc.shape, jnp.float32)
 
     to_log2 = DH ** (-0.5) * 1.4426950408889634
-    ones = jnp.ones((kv_ref.shape[1], DH), jnp.bfloat16)
     for h in range(head_count):
         seen = (frame <= frame_now) & (frame >= frame_now - sp_ref[2 + h])
 
@@ -46,22 +45,23 @@
             for c in range(kv_ref.shape[0]):
                 k = kv_ref[c, :, h * DH:(h + 1) * DH]
                 v = kv_ref[c, :, hd + h * DH:hd + (h + 1) * DH]
-                s = lax.dot_general(
-                    q, k, (((1,), (1,)), ((), ())), preferred_element_type=jnp.float32
+                st = lax.dot_general(
+                    k, q, (((1,), (1,)), ((), ())), preferred_element_type=jnp.float32
                 ) * to_log2
                 m_old = m_sc[h]
-                m_new = jnp.maximum(m_old, jnp.max(s, axis=1, keepdims=True))
+                m_new = jnp.maximum(m_old, jnp.max(st, axis=0, keepdims=True))
                 alpha = jnp.exp2(m_old - m_new)
-                p = jnp.exp2(s - m_new).astype(jnp.bfloat16)
-                total = jnp.dot(p, ones, preferred_element_type=jnp.float32)[:, :1]
-                l_sc[h] = alpha * l_sc[h] + total
-                acc_sc[h] = alpha * acc_sc[h] + jnp.dot(p, v, preferred_element_type=jnp.float32)
+                pt = jnp.exp2(st - m_new).astype(jnp.bfloat16)
+                l_sc[h] = alpha * l_sc[h] + jnp.sum(pt.astype(jnp.float32), axis=0, keepdims=True)
+                acc_sc[h] = alpha * acc_sc[h] + lax.dot_general(
+                    v, pt, (((0,), (0,)), ((), ())), preferred_element_type=jnp.float32
+                )
                 m_sc[h] = m_new
 
     @pl.when(step == pl.num_programs(0) - 1)
     def _():
         for h in range(head_count):
-            o_ref[:, h * DH:(h + 1) * DH] = (acc_sc[h] / l_sc[h]).astype(o_ref.dtype)
+            o_ref[:, h * DH:(h + 1) * DH] = (acc_sc[h] / l_sc[h]).T.astype(o_ref.dtype)
 
 
 def attend(scalars, queries, kv):
@@ -74,7 +74,7 @@
 
     flops = 4 * rows * parts * part_rows * hd * 6
     return pl.pallas_call(
-        functools.partial(attend_kernel, head_count, part_rows),
+        functools.partial(attend_kernel, head_count),
         out_shape=jax.ShapeDtypeStruct((rows, hd), jnp.bfloat16),
         grid_spec=pltpu.PrefetchScalarGridSpec(
             num_scalar_prefetch=1,
@@ -85,9 +85,9 @@
             ],
             out_specs=pl.BlockSpec((rows, hd), lambda step, sp: (0, 0)),
             scratch_shapes=[
-                pltpu.VMEM((head_count, rows, 1), jnp.float32),
-                pltpu.VMEM((head_count, rows, 1), jnp.float32),
-                pltpu.VMEM((head_count, rows, DH), jnp.float32),
+                pltpu.VMEM((head_count, 1, rows), jnp.float32),
+                pltpu.VMEM((head_count, 1, rows), jnp.float32),
+                pltpu.VMEM((head_count, DH, rows), jnp.float32),
             ],
         ),
         compiler_params=pltpu.CompilerParams(
@@ -141,7 +141,9 @@
         attended.reshape(shares, tokens_dev, attended.shape[1]), ("head", "dec"), 0, 0, tiled=False
     )
     mine = mine.transpose(1, 0, 2).reshape(tokens_dev, shares * attended.shape[1])
-    projected = jnp.dot(mine, weight_all, preferred_element_type=jnp.float32)
+    projected = lax.dot_general(
+        weight_all, mine, (((0,), (1,)), ((), ())), preferred_element_type=jnp.float32
+    ).T
     hidden = residual.astype(jnp.float32) + branch_gate[None, :] * projected
     center = jnp.mean(hidden, axis=1, keepdims=True)
     spread = jnp.mean((hidden - center) ** 2, axis=1, keepdims=True)

time: 202 us -> 201 us (level); the launches traced: 200 us -> 201 us
  no operation moved by 1% of the time
where the time goes in v4:
time: 201 us
  waiting for transfers between devices  118 us (59%)
  starting transfers between devices  36.9 us (18%)
  between operations  14.3 us (7%)
  local copies, waits for them, and re-layouts  10.9 us (5%)
  Pallas kernels  10.7 us (5%)
  matrix products  6.92 us (3%)
  other arithmetic  3.13 us (2%)
    all_gather x1, waiting for transfers between devices, per_device(): kv = lax.all_gather(kv, ('z', 'x', 'core'), axis=0, tiled=True)  107 us
    ppermute x4, starting transfers between devices, from_behind(): return lax.ppermute(x, axis, pairs)  26.6 us
    pallas_call x1, Pallas kernels, attend(): pl.pallas_call(functools.partial(attend_kernel, head_count), out_shape=ja...  10.7 us
    ppermute x4, waiting for transfers between devices, from_behind(): return lax.ppermute(x, axis, pairs)  7.9 us
    broadcast_in_dim x1, local copies, waits for them, and re-layouts, per_device(): jnp.broadcast_to(out_weight[None], (shares,) + out_weight.shape)  6.52 us
    all_to_all x1, starting transfers between devices, per_device(): lax.all_to_all(jnp.broadcast_to(out_weight[None], (shares,) + out_weight....  5.91 us
    dot_general x1, matrix products, per_device(): lax.dot_general(weight_all, mine, (((0,), (1,)), ((), ())), preferred_ele...  5.57 us
    all_to_all x1, starting transfers between devices, per_device(): lax.all_to_all(attended.reshape(shares, tokens_dev, attended.shape[1]), (...  4.36 us
  transfers between devices with their start and end apart: 7, of which 4 were waited for; matrix products, arithmetic and copies ran while one was open for 4% of the time, Pallas kernels for 5%

profile of v4, /device:TPU:63, one launch (start us, length us, event | category | flops | bytes accessed | tf_op | source)
XLA Modules:
  0.0 201.3 jit_solution(16555113146917747367)
XLA Ops:
  6.5 1.8 pad_maximum_fusion
  8.4 6.5 %broadcast_in_dim.2 = bf16[4,384,3072]{2,1,0:T(8,128)(2,1)} broadcast(bf16[384,3072]{1,0:T(8,128)(2,1)} %param.17), dimensions={1,2} | broadcast | bytes 11796480 | tf_op jit(solution)/shard_map/broadcast_in_dim | solution.py:137
  14.9 5.9 %all-to-all-start.1 = ((bf16[4,384,3072]{2,1,0:T(8,128)(2,1)}), bf16[4,384,3072]{2,1,0:T(8,128)(2,1)}, u32[]{:S(2)}, u32[]{:S(2)}) async-start(bf16[4,384,3072]{2,1,0:T(8,128)(2,1)} %broadcast_in_dim.2), calls=%async_computation.1 | async-start | bytes 18874368 | tf_op jit(solution)/shard_map/all_to_all | solution.py:136
  20.9 0.7 fusion.13
  22.3 107.1 %all-gather.2.cloned.1.call-done = bf16[16384,768]{1,0:T(8,128)(2,1)} async-done(((bf16[256,768]{1,0:T(8,128)(2,1)}), bf16[16384,768]{1,0:T(8,128)(2,1)}) %all-gather.2.cloned.1.call-update) | async-done | bytes 25165840 | tf_op jit(solution)/shard_map/all_gather | solution.py:130
  129.4 10.7 %shard_map.118 = bf16[256,384]{1,0:T(8,128)(2,1)} custom-call(s32[5]{0:T(128)S(1)} %pad_add_fusion.sp_ref, bf16[256,384]{1,0:T(8,128)(2,1)S(1)} %copy-done.1, bf16[1,8,2048,768]{3,2,1,0:T(8,128)(2,1)} %bitcast.51), custom_call_target="tpu_custom_call" | custom-call | flops 4831838208 | bytes 19267584 | tf_op jit(solution)/shard_map/pallas_call | solution.py:76
  140.1 4.4 %all-to-all-start = ((bf16[4,64,384]{2,1,0:T(8,128)(2,1)}), bf16[4,64,384]{2,1,0:T(8,128)(2,1)S(1)}, u32[]{:S(2)}, u32[]{:S(2)}) async-start(bf16[4,64,384]{2,1,0:T(8,128)(2,1)} %bitcast.3), calls=%async_computation | async-start | bytes 393216 | tf_op jit(solution)/shard_map/all_to_all | solution.py:140
  144.5 3.4 %all-to-all-done = bf16[4,64,384]{2,1,0:T(8,128)(2,1)S(1)} async-done(((bf16[4,64,384]{2,1,0:T(8,128)(2,1)}), bf16[4,64,384]{2,1,0:T(8,128)(2,1)S(1)}, u32[]{:S(2)}, u32[]{:S(2)}) %all-to-all-start) | async-done | bytes 196640 | tf_op jit(solution)/shard_map/all_to_all | solution.py:140
  147.9 5.6 %fusion.18 = (f32[64]{0:T(128)S(1)}, f32[64,3072]{1,0:T(8,128)S(1)}) fusion(bf16[4,384,3072]{2,1,0:T(8,128)(2,1)} %all-to-all-done.1, bf16[4,64,384]{2,1,0:T(8,128)(2,1)S(1)} %all-to-all-done, f32[3072]{0:T(1024)S(1)} %copy-done.3, bf16[64,3072]{1,0:T(8,128)(2,1)S(1)} %copy-done.2), kind=kOutput, calls=%fused_computation.37 | convolution fusion | flops 604766144 | bytes 10825984 | tf_op jit(solution)/shard_map/dot_general | solution.py:144
  153.5 0.3 multiply_reduce_fusion
  153.8 0.3 convolution_convert_fusion
  154.1 0.1 copy.17
  154.3 0.1 copy.18
  154.4 0.1 reshape.105
  154.6 11.3 %collective-permute-start = (bf16[1,1024]{1,0:T(2,128)(2,1)S(1)}, bf16[1,1024]{1,0:T(2,128)(2,1)S(1)}, u32[]{:S(2)}, u32[]{:S(2)}) collective-permute-start(bf16[1,1024]{1,0:T(2,128)(2,1)S(1)} %get-tuple-element.35), channel_id=1, source_target_pairs={{0,1},{1,2},{2,3},{3,4},{4,5},{5,6},{6,7},{7,8},{8,9},{9,10},{10,1... | collective-permute-start | bytes 6152 | tf_op jit(solution)/shard_map/ppermute | solution.py:22
  165.9 1.9 collective-permute-start.1
  167.9 7.1 %collective-permute-done.1 = bf16[1,1024]{1,0:T(2,128)(2,1)S(1)} collective-permute-done((bf16[1,1024]{1,0:T(2,128)(2,1)S(1)}, bf16[1,1024]{1,0:T(2,128)(2,1)S(1)}, u32[]{:S(2)}, u32[]{:S(2)}) %collective-permute-start.1) | collective-permute-done | bytes 2080 | tf_op jit(solution)/shard_map/ppermute | solution.py:22
  175.0 10.3 %collective-permute-start.2 = (bf16[6,1024]{1,0:T(8,128)(2,1)S(1)}, bf16[6,1024]{1,0:T(8,128)(2,1)S(1)}, u32[]{:S(2)}, u32[]{:S(2)}) collective-permute-start(bf16[6,1024]{1,0:T(8,128)(2,1)S(1)} %pad_maximum_fusion.3), channel_id=1, source_target_pairs={{0,64},{1,65},{2,66},{3,67},{4,68},{5,69},{6,70},{7,71},{8,72},{9,... | collective-permute-start | bytes 36872 | tf_op jit(solution)/shard_map/ppermute | solution.py:22
  185.4 3.1 %collective-permute-start.3 = (bf16[6,1024]{1,0:T(8,128)(2,1)S(1)}, bf16[6,1024]{1,0:T(8,128)(2,1)S(1)}, u32[]{:S(2)}, u32[]{:S(2)}) collective-permute-start(bf16[6,1024]{1,0:T(8,128)(2,1)S(1)} %pad_maximum_fusion.3), channel_id=1, source_target_pairs={{0,32},{1,33},{2,34},{3,35},{4,36},{5,37},{6,38},{7,39},{8,40},{9,... | collective-permute-start | bytes 36872 | tf_op jit(solution)/shard_map/ppermute | solution.py:22
  188.9 0.1 copy.40
  189.0 0.1 copy.48
  189.1 0.8 collective-permute-done.3
  189.9 0.1 stack.18
  190.0 0.1 copy.23
  190.2 0.1 stack.19
  190.3 0.1 copy.24
  190.4 0.1 fusion.9
  190.5 0.1 fusion.16
  190.6 0.1 copy.26
  190.8 0.1 copy.27
  190.9 0.1 copy.28
  191.0 0.1 copy.29
  191.1 0.1 copy.30
  191.2 0.1 copy.31
  191.3 0.1 copy.32
  191.4 0.1 copy.33
  191.5 0.1 copy.34
  191.6 0.1 copy.35
  191.7 0.1 copy.36
  191.8 0.1 copy.37
  191.9 0.1 copy.41
  192.0 0.1 copy.42
  192.1 0.1 copy.44
  192.3 0.1 copy.45
  192.4 0.1 copy.49
  192.5 0.1 copy.25
  192.6 0.8 concatenate.119
  193.5 1.0 fusion.2
  (41 shorter events, 0.9 us)
Async XLA Ops:
  6.5 186.9 %copy-start = (bf16[432,512]{1,0:T(8,128)(2,1)S(1)}, bf16[432,512]{1,0:T(8,128)(2,1)}, u32[]{:S(2)}) copy-start(bf16[432,512]{1,0:T(8,128)(2,1)} %param.22) | copy-start | bytes 1327108
  6.5 122.9 %all-gather.2.cloned.1.call-start = ((), (), s32[]{:S(2)}) async-start(), calls=%async_computation.2 | async-start | bytes 25559040 | tf_op jit(solution)/shard_map/all_gather | solution.py:130
  14.9 5.9 %copy-start.5 = (s32[12]{0:T(128)S(1)}, s32[12]{0:T(128)}, u32[]{:S(2)}) copy-start(s32[12]{0:T(128)} %param.15) | copy-start | bytes 148
  14.9 114.5 %copy-start.1 = (bf16[256,384]{1,0:T(8,128)(2,1)S(1)}, bf16[256,384]{1,0:T(8,128)(2,1)}, u32[]{:S(2)}) copy-start(bf16[256,384]{1,0:T(8,128)(2,1)} %q_ref.1) | copy-start | bytes 589828
  14.9 125.2 %all-to-all-start.1 = ((bf16[4,384,3072]{2,1,0:T(8,128)(2,1)}), bf16[4,384,3072]{2,1,0:T(8,128)(2,1)}, u32[]{:S(2)}, u32[]{:S(2)}) async-start(bf16[4,384,3072]{2,1,0:T(8,128)(2,1)} %broadcast_in_dim.2), calls=%async_computation.1 | async-start | bytes 18874368 | tf_op jit(solution)/shard_map/all_to_all | solution.py:136
  129.4 15.0 %copy-start.4 = (f32[3072]{0:T(1024)S(1)}, f32[3072]{0:T(1024)}, u32[]{:S(2)}) copy-start(f32[3072]{0:T(1024)} %param.20) | copy-start | bytes 36868
  129.4 18.5 %copy-start.2 = (bf16[64,3072]{1,0:T(8,128)(2,1)S(1)}, bf16[64,3072]{1,0:T(8,128)(2,1)}, u32[]{:S(2)}) copy-start(bf16[64,3072]{1,0:T(8,128)(2,1)} %param.16) | copy-start | bytes 1179652
  129.4 18.5 %copy-start.3 = (f32[3072]{0:T(1024)S(1)}, f32[3072]{0:T(1024)}, u32[]{:S(2)}) copy-start(f32[3072]{0:T(1024)} %param.18) | copy-start | bytes 36868
  140.1 13.7 %copy-start.6 = (bf16[3072,64]{0,1:T(8,128)(2,1)S(1)}, bf16[3072,64]{0,1:T(8,128)(2,1)}, u32[]{:S(2)}) copy-start(bf16[3072,64]{0,1:T(8,128)(2,1)} %param.21) | copy-start | bytes 1179652
  140.1 13.7 %copy-start.7 = (f32[3072]{0:T(1024)S(1)}, f32[3072]{0:T(1024)}, u32[]{:S(2)}) copy-start(f32[3072]{0:T(1024)} %param.19) | copy-start | bytes 36868
  140.1 7.8 %all-to-all-start = ((bf16[4,64,384]{2,1,0:T(8,128)(2,1)}), bf16[4,64,384]{2,1,0:T(8,128)(2,1)S(1)}, u32[]{:S(2)}, u32[]{:S(2)}) async-start(bf16[4,64,384]{2,1,0:T(8,128)(2,1)} %bitcast.3), calls=%async_computation | async-start | bytes 393216 | tf_op jit(solution)/shard_map/all_to_all | solution.py:140
  144.5 49.0 %copy-start.8 = (f32[512]{0:T(512)S(1)}, f32[512]{0:T(512)}, u32[]{:S(2)}) copy-start(f32[512]{0:T(512)} %param.23) | copy-start | bytes 6148
  154.6 13.3 %collective-permute-start = (bf16[1,1024]{1,0:T(2,128)(2,1)S(1)}, bf16[1,1024]{1,0:T(2,128)(2,1)S(1)}, u32[]{:S(2)}, u32[]{:S(2)}) collective-permute-start(bf16[1,1024]{1,0:T(2,128)(2,1)S(1)} %get-tuple-element.35), channel_id=1, source_target_pairs={{0,1},{1,2},{2,3},{3,4},{4,5},{5,6},{6,7},{7,8},{8,9},{9,10},{10,1... | collective-permute-start | bytes 6152 | tf_op jit(solution)/shard_map/ppermute | solution.py:22
  165.9 9.1 %collective-permute-start.1 = (bf16[1,1024]{1,0:T(2,128)(2,1)S(1)}, bf16[1,1024]{1,0:T(2,128)(2,1)S(1)}, u32[]{:S(2)}, u32[]{:S(2)}) collective-permute-start(bf16[1,1024]{1,0:T(2,128)(2,1)S(1)} %get-tuple-element.36), channel_id=1, source_target_pairs={{1,0},{2,1},{3,2},{4,3},{5,4},{6,5},{7,6},{8,7},{9,8},{10,9},{11,1... | collective-permute-start | bytes 6152 | tf_op jit(solution)/shard_map/ppermute | solution.py:22
  175.0 14.0 %collective-permute-start.2 = (bf16[6,1024]{1,0:T(8,128)(2,1)S(1)}, bf16[6,1024]{1,0:T(8,128)(2,1)S(1)}, u32[]{:S(2)}, u32[]{:S(2)}) collective-permute-start(bf16[6,1024]{1,0:T(8,128)(2,1)S(1)} %pad_maximum_fusion.3), channel_id=1, source_target_pairs={{0,64},{1,65},{2,66},{3,67},{4,68},{5,69},{6,70},{7,71},{8,72},{9,... | collective-permute-start | bytes 36872 | tf_op jit(solution)/shard_map/ppermute | solution.py:22
  185.4 4.5 %collective-permute-start.3 = (bf16[6,1024]{1,0:T(8,128)(2,1)S(1)}, bf16[6,1024]{1,0:T(8,128)(2,1)S(1)}, u32[]{:S(2)}, u32[]{:S(2)}) collective-permute-start(bf16[6,1024]{1,0:T(8,128)(2,1)S(1)} %pad_maximum_fusion.3), channel_id=1, source_target_pairs={{0,32},{1,33},{2,34},{3,35},{4,36},{5,37},{6,38},{7,39},{8,40},{9,... | collective-permute-start | bytes 36872 | tf_op jit(solution)/shard_map/ppermute | solution.py:22
Sparse Core Ops, SparseCore 0:
  10.1 119.2 all-gather.1

commit v5 on v4

--- a/solution.py
+++ b/solution.py
@@ -99,6 +99,36 @@
             bytes_accessed=parts * part_rows * width * 2 * 6 + rows * hd * 4,
         ),
     )(scalars, queries, kv)
+
+
+def project_kernel(w_ref, m_ref, o_ref):
+    @pl.when(pl.program_id(1) == 0)
+    def _():
+        o_ref[...] = jnp.zeros(o_ref.shape, jnp.float32)
+
+    o_ref[...] += jnp.dot(w_ref[...], m_ref[...], preferred_element_type=jnp.float32)
+
+
+def project(weight_t, mine_t):
+    parts, out_dim, in_dim = weight_t.shape
+    tokens = mine_t.shape[2]
+    block = 512
+    return pl.pallas_call(
+        project_kernel,
+        out_shape=jax.ShapeDtypeStruct((out_dim, tokens), jnp.float32),
+        grid=(out_dim // block, parts),
+        in_specs=[
+            pl.BlockSpec((None, block, in_dim), lambda i, j: (j, i, 0)),
+            pl.BlockSpec((None, in_dim, tokens), lambda i, j: (j, 0, 0)),
+        ],
+        out_specs=pl.BlockSpec((block, tokens), lambda i, j: (i, 0)),
+        compiler_params=pltpu.CompilerParams(dimension_semantics=("arbitrary", "arbitrary")),
+        cost_estimate=pl.CostEstimate(
+            flops=2 * parts * out_dim * in_dim * tokens,
+            transcendentals=0,
+            bytes_accessed=parts * (out_dim * in_dim * 2 + in_dim * tokens * 2) + out_dim * tokens * 4,
+        ),
+    )(weight_t, mine_t)
 
 
 def per_device(
@@ -129,21 +159,21 @@
     kv = jnp.concatenate([key_vectors, values], axis=1)
     kv = lax.all_gather(kv, ("z", "x", "core"), axis=0, tiled=True)
     kv = kv.reshape(1, FRAMES, kv.shape[0] // FRAMES, kv.shape[1])
+    shares = lax.axis_size(("head", "dec"))
+    weight_t = out_weight.T
+    weight_all = lax.all_to_all(
+        jnp.broadcast_to(weight_t[None], (shares,) + weight_t.shape), ("head", "dec"), 0, 0, tiled=False
+    )
+    kv, weight_all = lax.optimization_barrier((kv, weight_all))
     attended = attend(scalars, queries, kv)
 
     tokens_dev = slab_rows // lax.axis_size(("head", "dec"))
     shares = lax.axis_size(("head", "dec"))
-    weight_all = lax.all_to_all(
-        jnp.broadcast_to(out_weight[None], (shares,) + out_weight.shape),
-        ("head", "dec"), 0, 0, tiled=False,
-    ).reshape(shares * out_weight.shape[0], out_weight.shape[1])
     mine = lax.all_to_all(
         attended.reshape(shares, tokens_dev, attended.shape[1]), ("head", "dec"), 0, 0, tiled=False
     )
-    mine = mine.transpose(1, 0, 2).reshape(tokens_dev, shares * attended.shape[1])
-    projected = lax.dot_general(
-        weight_all, mine, (((0,), (1,)), ((), ())), preferred_element_type=jnp.float32
-    ).T
+    mine_t = mine.transpose(0, 2, 1)
+    projected = project(weight_all, mine_t).T
     hidden = residual.astype(jnp.float32) + branch_gate[None, :] * projected
     center = jnp.mean(hidden, axis=1, keepdims=True)
     spread = jnp.mean((hidden - center) ** 2, axis=1, keepdims=True)

time: 201 us -> 219 us (1.090)
  Pallas kernels: 10.7 us -> 27 us
  matrix products: 6.92 us -> 2.75 us
  local copies, waits for them, and re-layouts: 10.9 us -> 13.6 us
  other arithmetic: 3.13 us -> 5.41 us
    all_gather x1, waiting for transfers between devices: 107 us -> 4.92 us  [per_device(): kv = lax.all_gather(kv, ('z', 'x', 'core'), axis=0, tiled=True)]
    all_to_all x1, waiting for transfers between devices: 0.01 us -> 101 us  [per_device(): lax.all_to_all(jnp.broadcast_to(weight_t[None], (shares,) + weight_t.shap...]
    pallas_call x0 -> x1, Pallas kernels: none -> 17.5 us  [project(): pl.pallas_call(project_kernel, out_shape=jax.ShapeDtypeStruct((out_dim, t...]
    dot_general x1 -> x0, matrix products: 5.57 us -> none  [per_device(): lax.dot_general(weight_all, mine, (((0,), (1,)), ((), ())), preferred_ele...]
    transpose x0 -> x1, local copies, waits for them, and re-layouts: none -> 3 us  [per_device(): weight_t = out_weight.T]
  transfers between devices with their start and end apart: 7 -> 7, of which waited for: 4 -> 5; matrix products, arithmetic and copies ran while one was open for 4% -> 4% of each run, Pallas kernels for 5% -> 0%
where the time goes in v5:
time: 219 us; the launch traced here: 218 us
  waiting for transfers between devices  118 us (54%)
  starting transfers between devices  36.4 us (17%)
  Pallas kernels  27 us (12%)
  between operations  14.4 us (7%)
  local copies, waits for them, and re-layouts  13.6 us (6%)
  other arithmetic  5.41 us (2%)
  matrix products  2.75 us (1%)
    all_to_all x1, waiting for transfers between devices, per_device(): lax.all_to_all(jnp.broadcast_to(weight_t[None], (shares,) + weight_t.shap...  101 us
    ppermute x4, starting transfers between devices, from_behind(): return lax.ppermute(x, axis, pairs)  26.6 us
    pallas_call x1, Pallas kernels, project(): pl.pallas_call(project_kernel, out_shape=jax.ShapeDtypeStruct((out_dim, t...  17.5 us
    pallas_call x1, Pallas kernels, attend(): pl.pallas_call(functools.partial(attend_kernel, head_count), out_shape=ja...  9.5 us
    ppermute x4, waiting for transfers between devices, from_behind(): return lax.ppermute(x, axis, pairs)  7.89 us
    all_to_all x1, starting transfers between devices, per_device(): lax.all_to_all(jnp.broadcast_to(weight_t[None], (shares,) + weight_t.shap...  5.91 us
    all_gather x1, waiting for transfers between devices, per_device(): kv = lax.all_gather(kv, ('z', 'x', 'core'), axis=0, tiled=True)  4.92 us
    all_to_all x1, waiting for transfers between devices, per_device(): lax.all_to_all(attended.reshape(shares, tokens_dev, attended.shape[1]), (...  4.76 us
  transfers between devices with their start and end apart: 7, of which 5 were waited for; matrix products, arithmetic and copies ran while one was open for 4% of the time, Pallas kernels for 0%

profile of v5, /device:TPU:63, one launch (start us, length us, event | category | flops | bytes accessed | tf_op | source)
XLA Modules:
  0.0 218.0 jit_solution(5598002329092684987)
XLA Ops:
  6.5 1.8 pad_maximum_fusion
  8.4 3.0 %copy.23 = bf16[3072,384]{1,0:T(8,128)(2,1)S(1)} copy(bf16[3072,384]{0,1:T(8,128)(2,1)} %bitcast.51) | data formatting | bytes 4718592 | tf_op jit(solution)/shard_map/transpose | solution.py:163
  11.4 4.5 %broadcast_in_dim.2 = bf16[4,3072,384]{2,1,0:T(8,128)(2,1)} broadcast(bf16[3072,384]{1,0:T(8,128)(2,1)S(1)} %copy.23), dimensions={1,2} | broadcast | bytes 11796480 | tf_op jit(solution)/shard_map/broadcast_in_dim | solution.py:165
  15.9 5.9 %all-to-all-start = ((bf16[4,3072,384]{2,1,0:T(8,128)(2,1)}), bf16[4,3072,384]{2,1,0:T(8,128)(2,1)}, u32[]{:S(2)}, u32[]{:S(2)}) async-start(bf16[4,3072,384]{2,1,0:T(8,128)(2,1)} %broadcast_in_dim.2), calls=%async_computation | async-start | bytes 18874368 | tf_op jit(solution)/shard_map/all_to_all | solution.py:164
  21.8 0.7 fusion.7
  23.2 0.4 copy.22
  23.6 100.9 %all-to-all-done.w_ref = bf16[4,3072,384]{2,1,0:T(8,128)(2,1)} async-done(((bf16[4,3072,384]{2,1,0:T(8,128)(2,1)}), bf16[4,3072,384]{2,1,0:T(8,128)(2,1)}, u32[]{:S(2)}, u32[]{:S(2)}) %all-to-all-start) | async-done | bytes 9437216 | tf_op jit(solution)/shard_map/all_to_all | solution.py:164
  124.5 4.9 %all-gather.2.cloned.1.call-done = bf16[16384,768]{1,0:T(8,128)(2,1)} async-done(((bf16[256,768]{1,0:T(8,128)(2,1)}), bf16[16384,768]{1,0:T(8,128)(2,1)}) %all-gather.2.cloned.1.call-update) | async-done | bytes 25165840 | tf_op jit(solution)/shard_map/all_gather | solution.py:160
  129.4 9.5 %shard_map.118 = bf16[256,384]{1,0:T(8,128)(2,1)} custom-call(s32[5]{0:T(128)S(1)} %pad_add_fusion.sp_ref, bf16[256,384]{1,0:T(8,128)(2,1)S(1)} %copy-done.1, bf16[1,8,2048,768]{3,2,1,0:T(8,128)(2,1)} %bitcast.50), custom_call_target="tpu_custom_call" | custom-call | flops 4831838208 | bytes 19267584 | tf_op jit(solution)/shard_map/pallas_call | solution.py:76
  138.9 3.9 %all-to-all-start.1 = ((bf16[4,64,384]{2,1,0:T(8,128)(2,1)}), bf16[4,64,384]{2,1,0:T(8,128)(2,1)S(1)}, u32[]{:S(2)}, u32[]{:S(2)}) async-start(bf16[4,64,384]{2,1,0:T(8,128)(2,1)} %bitcast.4), calls=%async_computation.1 | async-start | bytes 393216 | tf_op jit(solution)/shard_map/all_to_all | solution.py:172
  142.9 4.8 %all-to-all-done.1 = bf16[4,64,384]{2,1,0:T(8,128)(2,1)S(1)} async-done(((bf16[4,64,384]{2,1,0:T(8,128)(2,1)}), bf16[4,64,384]{2,1,0:T(8,128)(2,1)S(1)}, u32[]{:S(2)}, u32[]{:S(2)}) %all-to-all-start.1) | async-done | bytes 196640 | tf_op jit(solution)/shard_map/all_to_all | solution.py:172
  147.6 0.9 copy.24
  148.6 17.5 %shard_map.119 = f32[3072,64]{1,0:T(8,128)} custom-call(bf16[4,3072,384]{2,1,0:T(8,128)(2,1)} %all-to-all-done.w_ref, bf16[4,384,64]{2,1,0:T(8,128)(2,1)} %bitcast.52), custom_call_target="tpu_custom_call" | custom-call | flops 603979776 | bytes 10420224 | tf_op jit(solution)/shard_map/pallas_call | solution.py:116
  166.0 2.0 fusion.6
  168.1 0.5 multiply_reduce_fusion
  168.6 0.4 copy-done.7
  169.0 1.8 convolution_convert_fusion
  171.0 0.1 copy.26
  171.1 0.1 reshape.103
  171.3 10.1 %collective-permute-start = (bf16[1,1024]{1,0:T(2,128)(2,1)S(1)}, bf16[1,1024]{1,0:T(2,128)(2,1)S(1)}, u32[]{:S(2)}, u32[]{:S(2)}) collective-permute-start(bf16[1,1024]{1,0:T(2,128)(2,1)S(1)} %get-tuple-element.39), channel_id=1, source_target_pairs={{0,1},{1,2},{2,3},{3,4},{4,5},{5,6},{6,7},{7,8},{8,9},{9,10},{10,1... | collective-permute-start | bytes 6152 | tf_op jit(solution)/shard_map/ppermute | solution.py:22
  181.4 1.9 collective-permute-start.1
  183.4 7.1 %collective-permute-done.1 = bf16[1,1024]{1,0:T(2,128)(2,1)S(1)} collective-permute-done((bf16[1,1024]{1,0:T(2,128)(2,1)S(1)}, bf16[1,1024]{1,0:T(2,128)(2,1)S(1)}, u32[]{:S(2)}, u32[]{:S(2)}) %collective-permute-start.1) | collective-permute-done | bytes 2080 | tf_op jit(solution)/shard_map/ppermute | solution.py:22
  190.6 11.5 %collective-permute-start.2 = (bf16[6,1024]{1,0:T(8,128)(2,1)S(1)}, bf16[6,1024]{1,0:T(8,128)(2,1)S(1)}, u32[]{:S(2)}, u32[]{:S(2)}) collective-permute-start(bf16[6,1024]{1,0:T(8,128)(2,1)S(1)} %pad_maximum_fusion.3), channel_id=1, source_target_pairs={{0,64},{1,65},{2,66},{3,67},{4,68},{5,69},{6,70},{7,71},{8,72},{9,... | collective-permute-start | bytes 36872 | tf_op jit(solution)/shard_map/ppermute | solution.py:22
  202.0 3.1 %collective-permute-start.3 = (bf16[6,1024]{1,0:T(8,128)(2,1)S(1)}, bf16[6,1024]{1,0:T(8,128)(2,1)S(1)}, u32[]{:S(2)}, u32[]{:S(2)}) collective-permute-start(bf16[6,1024]{1,0:T(8,128)(2,1)S(1)} %pad_maximum_fusion.3), channel_id=1, source_target_pairs={{0,32},{1,33},{2,34},{3,35},{4,36},{5,37},{6,38},{7,39},{8,40},{9,... | collective-permute-start | bytes 36872 | tf_op jit(solution)/shard_map/ppermute | solution.py:22
  205.5 0.1 copy.48
  205.6 0.1 copy.56
  205.8 0.8 collective-permute-done.3
  206.6 0.1 stack.18
  206.8 0.1 stack.19
  207.2 0.1 fusion.10
  207.3 0.1 copy.34
  207.4 0.1 copy.35
  207.5 0.1 copy.36
  207.6 0.1 copy.37
  207.7 0.1 copy.38
  207.9 0.1 copy.39
  208.1 0.1 copy.41
  208.2 0.1 copy.42
  208.3 0.1 copy.43
  208.4 0.1 copy.44
  208.5 0.1 copy.45
  208.6 0.1 copy.49
  208.7 0.1 copy.50
  208.8 0.1 copy.52
  208.9 0.1 copy.53
  209.1 0.1 copy.33
  209.3 0.8 concatenate.119
  210.1 1.0 fusion
  (47 shorter events, 1.4 us)
Async XLA Ops:
  6.5 203.6 %copy-start = (bf16[432,512]{1,0:T(8,128)(2,1)S(1)}, bf16[432,512]{1,0:T(8,128)(2,1)}, u32[]{:S(2)}) copy-start(bf16[432,512]{1,0:T(8,128)(2,1)} %param.22) | copy-start | bytes 1327108
  6.5 122.9 %all-gather.2.cloned.1.call-start = ((), (), s32[]{:S(2)}) async-start(), calls=%async_computation.2 | async-start | bytes 25559040 | tf_op jit(solution)/shard_map/all_gather | solution.py:160
  15.9 5.9 %copy-start.6 = (s32[12]{0:T(128)S(1)}, s32[12]{0:T(128)}, u32[]{:S(2)}) copy-start(s32[12]{0:T(128)} %param.15) | copy-start | bytes 148
  15.9 7.3 %copy-start.3 = (bf16[64,3072]{1,0:T(8,128)(2,1)S(1)}, bf16[64,3072]{1,0:T(8,128)(2,1)}, u32[]{:S(2)}) copy-start(bf16[64,3072]{1,0:T(8,128)(2,1)} %param.16) | copy-start | bytes 1179652
  15.9 113.5 %copy-start.1 = (bf16[256,384]{1,0:T(8,128)(2,1)S(1)}, bf16[256,384]{1,0:T(8,128)(2,1)}, u32[]{:S(2)}) copy-start(bf16[256,384]{1,0:T(8,128)(2,1)} %q_ref.1) | copy-start | bytes 589828
  15.9 108.6 %all-to-all-start = ((bf16[4,3072,384]{2,1,0:T(8,128)(2,1)}), bf16[4,3072,384]{2,1,0:T(8,128)(2,1)}, u32[]{:S(2)}, u32[]{:S(2)}) async-start(bf16[4,3072,384]{2,1,0:T(8,128)(2,1)} %broadcast_in_dim.2), calls=%async_computation | async-start | bytes 18874368 | tf_op jit(solution)/shard_map/all_to_all | solution.py:164
  129.4 13.5 %copy-start.5 = (f32[3072]{0:T(1024)S(1)}, f32[3072]{0:T(1024)}, u32[]{:S(2)}) copy-start(f32[3072]{0:T(1024)} %param.20) | copy-start | bytes 36868
  138.9 8.7 %all-to-all-start.1 = ((bf16[4,64,384]{2,1,0:T(8,128)(2,1)}), bf16[4,64,384]{2,1,0:T(8,128)(2,1)S(1)}, u32[]{:S(2)}, u32[]{:S(2)}) async-start(bf16[4,64,384]{2,1,0:T(8,128)(2,1)} %bitcast.4), calls=%async_computation.1 | async-start | bytes 393216 | tf_op jit(solution)/shard_map/all_to_all | solution.py:172
  148.6 17.5 %copy-start.4 = (f32[3072]{0:T(1024)S(1)}, f32[3072]{0:T(1024)}, u32[]{:S(2)}) copy-start(f32[3072]{0:T(1024)} %param.18) | copy-start | bytes 36868
  166.0 2.0 copy-start.2
  168.0 1.0 copy-start.7
  168.1 1.0 copy-start.8
  171.3 12.2 %collective-permute-start = (bf16[1,1024]{1,0:T(2,128)(2,1)S(1)}, bf16[1,1024]{1,0:T(2,128)(2,1)S(1)}, u32[]{:S(2)}, u32[]{:S(2)}) collective-permute-start(bf16[1,1024]{1,0:T(2,128)(2,1)S(1)} %get-tuple-element.39), channel_id=1, source_target_pairs={{0,1},{1,2},{2,3},{3,4},{4,5},{5,6},{6,7},{7,8},{8,9},{9,10},{10,1... | collective-permute-start | bytes 6152 | tf_op jit(solution)/shard_map/ppermute | solution.py:22
  181.4 9.1 %collective-permute-start.1 = (bf16[1,1024]{1,0:T(2,128)(2,1)S(1)}, bf16[1,1024]{1,0:T(2,128)(2,1)S(1)}, u32[]{:S(2)}, u32[]{:S(2)}) collective-permute-start(bf16[1,1024]{1,0:T(2,128)(2,1)S(1)} %get-tuple-element.40), channel_id=1, source_target_pairs={{1,0},{2,1},{3,2},{4,3},{5,4},{6,5},{7,6},{8,7},{9,8},{10,9},{11,1... | collective-permute-start | bytes 6152 | tf_op jit(solution)/shard_map/ppermute | solution.py:22
  190.6 15.2 %collective-permute-start.2 = (bf16[6,1024]{1,0:T(8,128)(2,1)S(1)}, bf16[6,1024]{1,0:T(8,128)(2,1)S(1)}, u32[]{:S(2)}, u32[]{:S(2)}) collective-permute-start(bf16[6,1024]{1,0:T(8,128)(2,1)S(1)} %pad_maximum_fusion.3), channel_id=1, source_target_pairs={{0,64},{1,65},{2,66},{3,67},{4,68},{5,69},{6,70},{7,71},{8,72},{9,... | collective-permute-start | bytes 36872 | tf_op jit(solution)/shard_map/ppermute | solution.py:22
  202.0 4.5 %collective-permute-start.3 = (bf16[6,1024]{1,0:T(8,128)(2,1)S(1)}, bf16[6,1024]{1,0:T(8,128)(2,1)S(1)}, u32[]{:S(2)}, u32[]{:S(2)}) collective-permute-start(bf16[6,1024]{1,0:T(8,128)(2,1)S(1)} %pad_maximum_fusion.3), channel_id=1, source_target_pairs={{0,32},{1,33},{2,34},{3,35},{4,36},{5,37},{6,38},{7,39},{8,40},{9,... | collective-permute-start | bytes 36872 | tf_op jit(solution)/shard_map/ppermute | solution.py:22
  207.8 2.3 %copy-start.9 = (f32[512]{0:T(512)S(1)}, f32[512]{0:T(512)}, u32[]{:S(2)}) copy-start(f32[512]{0:T(512)} %param.23) | copy-start | bytes 6148
Sparse Core Ops, SparseCore 0:
  10.1 119.2 all-gather.1

commit v6 on v4

--- a/solution.py
+++ b/solution.py
@@ -12,6 +12,7 @@
 LC = 16
 FRAMES = 8
 PW = 32
+WINDOW = 5
 
 ROWS = ("z", "x", "core", "head", "dec")
 
@@ -78,7 +79,7 @@
         out_shape=jax.ShapeDtypeStruct((rows, hd), jnp.bfloat16),
         grid_spec=pltpu.PrefetchScalarGridSpec(
             num_scalar_prefetch=1,
-            grid=(frames,),
+            grid=(min(frames, WINDOW + 1),),
             in_specs=[
                 pl.BlockSpec((rows, hd), lambda step, sp: (0, 0)),
                 pl.BlockSpec((parts, None, part_rows, width), kv_map),

time: 201 us -> 200 us (level)
  starting transfers between devices: 36.9 us -> 34.2 us
    ppermute x4, starting transfers between devices: 26.6 us -> 24.2 us  [from_behind(): return lax.ppermute(x, axis, pairs)]
where the time goes in v6:
time: 200 us; the launch traced here: 198 us
  waiting for transfers between devices  118 us (59%)
  starting transfers between devices  34.2 us (17%)
  between operations  14.3 us (7%)
  local copies, waits for them, and re-layouts  10.9 us (5%)
  Pallas kernels  10.5 us (5%)
  matrix products  6.91 us (3%)
  other arithmetic  3.13 us (2%)
    all_gather x1, waiting for transfers between devices, per_device(): kv = lax.all_gather(kv, ('z', 'x', 'core'), axis=0, tiled=True)  107 us
    ppermute x4, starting transfers between devices, from_behind(): return lax.ppermute(x, axis, pairs)  24.2 us
    pallas_call x1, Pallas kernels, attend(): pl.pallas_call(functools.partial(attend_kernel, head_count), out_shape=ja...  10.5 us
    ppermute x4, waiting for transfers between devices, from_behind(): return lax.ppermute(x, axis, pairs)  7.83 us
    broadcast_in_dim x1, local copies, waits for them, and re-layouts, per_device(): jnp.broadcast_to(out_weight[None], (shares,) + out_weight.shape)  6.52 us
    all_to_all x1, starting transfers between devices, per_device(): lax.all_to_all(jnp.broadcast_to(out_weight[None], (shares,) + out_weight....  5.91 us
    dot_general x1, matrix products, per_device(): lax.dot_general(weight_all, mine, (((0,), (1,)), ((), ())), preferred_ele...  5.57 us
    all_to_all x1, starting transfers between devices, per_device(): lax.all_to_all(attended.reshape(shares, tokens_dev, attended.shape[1]), (...  4.09 us
  transfers between devices with their start and end apart: 7, of which 4 were waited for; matrix products, arithmetic and copies ran while one was open for 4% of the time, Pallas kernels for 5%

profile of v6, /device:TPU:63, one launch (start us, length us, event | category | flops | bytes accessed | tf_op | source)
XLA Modules:
  0.0 198.5 jit_solution(1615815519307668816)
XLA Ops:
  6.5 1.8 pad_maximum_fusion
  8.4 6.5 %broadcast_in_dim.2 = bf16[4,384,3072]{2,1,0:T(8,128)(2,1)} broadcast(bf16[384,3072]{1,0:T(8,128)(2,1)} %param.17), dimensions={1,2} | broadcast | bytes 11796480 | tf_op jit(solution)/shard_map/broadcast_in_dim | solution.py:138
  14.9 5.9 %all-to-all-start.1 = ((bf16[4,384,3072]{2,1,0:T(8,128)(2,1)}), bf16[4,384,3072]{2,1,0:T(8,128)(2,1)}, u32[]{:S(2)}, u32[]{:S(2)}) async-start(bf16[4,384,3072]{2,1,0:T(8,128)(2,1)} %broadcast_in_dim.2), calls=%async_computation.1 | async-start | bytes 18874368 | tf_op jit(solution)/shard_map/all_to_all | solution.py:137
  20.9 0.7 fusion.13
  22.3 107.1 %all-gather.2.cloned.1.call-done = bf16[16384,768]{1,0:T(8,128)(2,1)} async-done(((bf16[256,768]{1,0:T(8,128)(2,1)}), bf16[16384,768]{1,0:T(8,128)(2,1)}) %all-gather.2.cloned.1.call-update) | async-done | bytes 25165840 | tf_op jit(solution)/shard_map/all_gather | solution.py:131
  129.4 10.5 %shard_map.118 = bf16[256,384]{1,0:T(8,128)(2,1)} custom-call(s32[5]{0:T(128)S(1)} %pad_add_fusion.sp_ref, bf16[256,384]{1,0:T(8,128)(2,1)S(1)} %copy-done.1, bf16[1,8,2048,768]{3,2,1,0:T(8,128)(2,1)} %bitcast.51), custom_call_target="tpu_custom_call" | custom-call | flops 4831838208 | bytes 19267584 | tf_op jit(solution)/shard_map/pallas_call | solution.py:77
  140.0 4.1 %all-to-all-start = ((bf16[4,64,384]{2,1,0:T(8,128)(2,1)}), bf16[4,64,384]{2,1,0:T(8,128)(2,1)S(1)}, u32[]{:S(2)}, u32[]{:S(2)}) async-start(bf16[4,64,384]{2,1,0:T(8,128)(2,1)} %bitcast.3), calls=%async_computation | async-start | bytes 393216 | tf_op jit(solution)/shard_map/all_to_all | solution.py:141
  144.1 3.4 %all-to-all-done = bf16[4,64,384]{2,1,0:T(8,128)(2,1)S(1)} async-done(((bf16[4,64,384]{2,1,0:T(8,128)(2,1)}), bf16[4,64,384]{2,1,0:T(8,128)(2,1)S(1)}, u32[]{:S(2)}, u32[]{:S(2)}) %all-to-all-start) | async-done | bytes 196640 | tf_op jit(solution)/shard_map/all_to_all | solution.py:141
  147.5 5.6 %fusion.18 = (f32[64]{0:T(128)S(1)}, f32[64,3072]{1,0:T(8,128)S(1)}) fusion(bf16[4,384,3072]{2,1,0:T(8,128)(2,1)} %all-to-all-done.1, bf16[4,64,384]{2,1,0:T(8,128)(2,1)S(1)} %all-to-all-done, f32[3072]{0:T(1024)S(1)} %copy-done.3, bf16[64,3072]{1,0:T(8,128)(2,1)S(1)} %copy-done.2), kind=kOutput, calls=%fused_computation.37 | convolution fusion | flops 604766144 | bytes 10825984 | tf_op jit(solution)/shard_map/dot_general | solution.py:145
  153.1 0.3 multiply_reduce_fusion
  153.4 0.3 convolution_convert_fusion
  153.7 0.1 copy.17
  153.9 0.1 copy.18
  154.1 0.1 reshape.105
  154.2 11.2 %collective-permute-start = (bf16[1,1024]{1,0:T(2,128)(2,1)S(1)}, bf16[1,1024]{1,0:T(2,128)(2,1)S(1)}, u32[]{:S(2)}, u32[]{:S(2)}) collective-permute-start(bf16[1,1024]{1,0:T(2,128)(2,1)S(1)} %get-tuple-element.35), channel_id=1, source_target_pairs={{0,1},{1,2},{2,3},{3,4},{4,5},{5,6},{6,7},{7,8},{8,9},{9,10},{10,1... | collective-permute-start | bytes 6152 | tf_op jit(solution)/shard_map/ppermute | solution.py:23
  165.4 1.9 collective-permute-start.1
  167.4 7.1 %collective-permute-done.1 = bf16[1,1024]{1,0:T(2,128)(2,1)S(1)} collective-permute-done((bf16[1,1024]{1,0:T(2,128)(2,1)S(1)}, bf16[1,1024]{1,0:T(2,128)(2,1)S(1)}, u32[]{:S(2)}, u32[]{:S(2)}) %collective-permute-start.1) | collective-permute-done | bytes 2080 | tf_op jit(solution)/shard_map/ppermute | solution.py:23
  174.5 8.0 %collective-permute-start.2 = (bf16[6,1024]{1,0:T(8,128)(2,1)S(1)}, bf16[6,1024]{1,0:T(8,128)(2,1)S(1)}, u32[]{:S(2)}, u32[]{:S(2)}) collective-permute-start(bf16[6,1024]{1,0:T(8,128)(2,1)S(1)} %pad_maximum_fusion.3), channel_id=1, source_target_pairs={{0,64},{1,65},{2,66},{3,67},{4,68},{5,69},{6,70},{7,71},{8,72},{9,... | collective-permute-start | bytes 36872 | tf_op jit(solution)/shard_map/ppermute | solution.py:23
  182.5 3.1 %collective-permute-start.3 = (bf16[6,1024]{1,0:T(8,128)(2,1)S(1)}, bf16[6,1024]{1,0:T(8,128)(2,1)S(1)}, u32[]{:S(2)}, u32[]{:S(2)}) collective-permute-start(bf16[6,1024]{1,0:T(8,128)(2,1)S(1)} %pad_maximum_fusion.3), channel_id=1, source_target_pairs={{0,32},{1,33},{2,34},{3,35},{4,36},{5,37},{6,38},{7,39},{8,40},{9,... | collective-permute-start | bytes 36872 | tf_op jit(solution)/shard_map/ppermute | solution.py:23
  186.1 0.1 copy.40
  186.2 0.1 copy.48
  186.3 0.7 collective-permute-done.3
  187.1 0.1 stack.18
  187.2 0.1 copy.23
  187.3 0.1 stack.19
  187.5 0.1 copy.24
  187.6 0.1 fusion.9
  187.7 0.1 fusion.16
  187.8 0.1 copy.26
  187.9 0.1 copy.27
  188.0 0.1 copy.28
  188.1 0.1 copy.29
  188.2 0.1 copy.30
  188.4 0.1 copy.31
  188.5 0.1 copy.32
  188.6 0.1 copy.33
  188.7 0.1 copy.34
  188.8 0.1 copy.35
  188.9 0.1 copy.36
  189.0 0.1 copy.37
  189.1 0.1 copy.41
  189.2 0.1 copy.42
  189.3 0.1 copy.44
  189.4 0.1 copy.45
  189.5 0.1 copy.49
  189.6 0.1 copy.25
  189.8 0.8 concatenate.119
  190.6 1.0 fusion.2
  (41 shorter events, 0.9 us)
Async XLA Ops:
  6.5 184.1 %copy-start = (bf16[432,512]{1,0:T(8,128)(2,1)S(1)}, bf16[432,512]{1,0:T(8,128)(2,1)}, u32[]{:S(2)}) copy-start(bf16[432,512]{1,0:T(8,128)(2,1)} %param.22) | copy-start | bytes 1327108
  6.5 122.9 %all-gather.2.cloned.1.call-start = ((), (), s32[]{:S(2)}) async-start(), calls=%async_computation.2 | async-start | bytes 25559040 | tf_op jit(solution)/shard_map/all_gather | solution.py:131
  14.9 5.9 %copy-start.5 = (s32[12]{0:T(128)S(1)}, s32[12]{0:T(128)}, u32[]{:S(2)}) copy-start(s32[12]{0:T(128)} %param.15) | copy-start | bytes 148
  14.9 114.5 %copy-start.1 = (bf16[256,384]{1,0:T(8,128)(2,1)S(1)}, bf16[256,384]{1,0:T(8,128)(2,1)}, u32[]{:S(2)}) copy-start(bf16[256,384]{1,0:T(8,128)(2,1)} %q_ref.1) | copy-start | bytes 589828
  14.9 125.1 %all-to-all-start.1 = ((bf16[4,384,3072]{2,1,0:T(8,128)(2,1)}), bf16[4,384,3072]{2,1,0:T(8,128)(2,1)}, u32[]{:S(2)}, u32[]{:S(2)}) async-start(bf16[4,384,3072]{2,1,0:T(8,128)(2,1)} %broadcast_in_dim.2), calls=%async_computation.1 | async-start | bytes 18874368 | tf_op jit(solution)/shard_map/all_to_all | solution.py:137
  129.4 14.7 %copy-start.4 = (f32[3072]{0:T(1024)S(1)}, f32[3072]{0:T(1024)}, u32[]{:S(2)}) copy-start(f32[3072]{0:T(1024)} %param.20) | copy-start | bytes 36868
  129.4 18.1 %copy-start.2 = (bf16[64,3072]{1,0:T(8,128)(2,1)S(1)}, bf16[64,3072]{1,0:T(8,128)(2,1)}, u32[]{:S(2)}) copy-start(bf16[64,3072]{1,0:T(8,128)(2,1)} %param.16) | copy-start | bytes 1179652
  129.4 18.1 %copy-start.3 = (f32[3072]{0:T(1024)S(1)}, f32[3072]{0:T(1024)}, u32[]{:S(2)}) copy-start(f32[3072]{0:T(1024)} %param.18) | copy-start | bytes 36868
  140.0 13.4 %copy-start.6 = (bf16[3072,64]{0,1:T(8,128)(2,1)S(1)}, bf16[3072,64]{0,1:T(8,128)(2,1)}, u32[]{:S(2)}) copy-start(bf16[3072,64]{0,1:T(8,128)(2,1)} %param.21) | copy-start | bytes 1179652
  140.0 13.4 %copy-start.7 = (f32[3072]{0:T(1024)S(1)}, f32[3072]{0:T(1024)}, u32[]{:S(2)}) copy-start(f32[3072]{0:T(1024)} %param.19) | copy-start | bytes 36868
  140.0 7.5 %all-to-all-start = ((bf16[4,64,384]{2,1,0:T(8,128)(2,1)}), bf16[4,64,384]{2,1,0:T(8,128)(2,1)S(1)}, u32[]{:S(2)}, u32[]{:S(2)}) async-start(bf16[4,64,384]{2,1,0:T(8,128)(2,1)} %bitcast.3), calls=%async_computation | async-start | bytes 393216 | tf_op jit(solution)/shard_map/all_to_all | solution.py:141
  144.1 46.5 %copy-start.8 = (f32[512]{0:T(512)S(1)}, f32[512]{0:T(512)}, u32[]{:S(2)}) copy-start(f32[512]{0:T(512)} %param.23) | copy-start | bytes 6148
  154.2 13.2 %collective-permute-start = (bf16[1,1024]{1,0:T(2,128)(2,1)S(1)}, bf16[1,1024]{1,0:T(2,128)(2,1)S(1)}, u32[]{:S(2)}, u32[]{:S(2)}) collective-permute-start(bf16[1,1024]{1,0:T(2,128)(2,1)S(1)} %get-tuple-element.35), channel_id=1, source_target_pairs={{0,1},{1,2},{2,3},{3,4},{4,5},{5,6},{6,7},{7,8},{8,9},{9,10},{10,1... | collective-permute-start | bytes 6152 | tf_op jit(solution)/shard_map/ppermute | solution.py:23
  165.4 9.1 %collective-permute-start.1 = (bf16[1,1024]{1,0:T(2,128)(2,1)S(1)}, bf16[1,1024]{1,0:T(2,128)(2,1)S(1)}, u32[]{:S(2)}, u32[]{:S(2)}) collective-permute-start(bf16[1,1024]{1,0:T(2,128)(2,1)S(1)} %get-tuple-element.36), channel_id=1, source_target_pairs={{1,0},{2,1},{3,2},{4,3},{5,4},{6,5},{7,6},{8,7},{9,8},{10,9},{11,1... | collective-permute-start | bytes 6152 | tf_op jit(solution)/shard_map/ppermute | solution.py:23
  174.5 11.8 %collective-permute-start.2 = (bf16[6,1024]{1,0:T(8,128)(2,1)S(1)}, bf16[6,1024]{1,0:T(8,128)(2,1)S(1)}, u32[]{:S(2)}, u32[]{:S(2)}) collective-permute-start(bf16[6,1024]{1,0:T(8,128)(2,1)S(1)} %pad_maximum_fusion.3), channel_id=1, source_target_pairs={{0,64},{1,65},{2,66},{3,67},{4,68},{5,69},{6,70},{7,71},{8,72},{9,... | collective-permute-start | bytes 36872 | tf_op jit(solution)/shard_map/ppermute | solution.py:23
  182.5 4.5 %collective-permute-start.3 = (bf16[6,1024]{1,0:T(8,128)(2,1)S(1)}, bf16[6,1024]{1,0:T(8,128)(2,1)S(1)}, u32[]{:S(2)}, u32[]{:S(2)}) collective-permute-start(bf16[6,1024]{1,0:T(8,128)(2,1)S(1)} %pad_maximum_fusion.3), channel_id=1, source_target_pairs={{0,32},{1,33},{2,34},{3,35},{4,36},{5,37},{6,38},{7,39},{8,40},{9,... | collective-permute-start | bytes 36872 | tf_op jit(solution)/shard_map/ppermute | solution.py:23
Sparse Core Ops, SparseCore 0:
  10.1 119.2 all-gather.1

commit v7 on v4

--- a/solution.py
+++ b/solution.py
@@ -42,9 +42,9 @@
         @pl.when(seen)
         def _():
             q = q_ref[:, h * DH:(h + 1) * DH]
-            for c in range(kv_ref.shape[0]):
-                k = kv_ref[c, :, h * DH:(h + 1) * DH]
-                v = kv_ref[c, :, hd + h * DH:hd + (h + 1) * DH]
+            for c in range(1):
+                k = kv_ref[0, :, h * DH:(h + 1) * DH]
+                v = kv_ref[1, :, h * DH:(h + 1) * DH]
                 st = lax.dot_general(
                     k, q, (((1,), (1,)), ((), ())), preferred_element_type=jnp.float32
                 ) * to_log2
@@ -72,7 +72,7 @@
     def kv_map(step, sp):
         return (0, jnp.minimum(sp[1] + step, sp[0]), 0, 0)
 
-    flops = 4 * rows * parts * part_rows * hd * 6
+    flops = 4 * rows * part_rows * hd * 6
     return pl.pallas_call(
         functools.partial(attend_kernel, head_count),
         out_shape=jax.ShapeDtypeStruct((rows, hd), jnp.bfloat16),
@@ -95,7 +95,7 @@
         ),
         cost_estimate=pl.CostEstimate(
             flops=flops,
-            transcendentals=rows * parts * part_rows * head_count * 6,
+            transcendentals=rows * part_rows * head_count * 6,
             bytes_accessed=parts * part_rows * width * 2 * 6 + rows * hd * 4,
         ),
     )(scalars, queries, kv)
@@ -126,9 +126,9 @@
         [jnp.stack([frame_index, first_frame]).astype(jnp.int32), lookback_heads.astype(jnp.int32)]
     )
 
-    kv = jnp.concatenate([key_vectors, values], axis=1)
-    kv = lax.all_gather(kv, ("z", "x", "core"), axis=0, tiled=True)
-    kv = kv.reshape(1, FRAMES, kv.shape[0] // FRAMES, kv.shape[1])
+    kv = jnp.stack([key_vectors, values])
+    kv = lax.all_gather(kv, ("z", "x", "core"), axis=1, tiled=True)
+    kv = kv.reshape(2, FRAMES, kv.shape[1] // FRAMES, kv.shape[2])
     attended = attend(scalars, queries, kv)
 
     tokens_dev = slab_rows // lax.axis_size(("head", "dec"))

time: 201 us -> 202 us (level)
  no operation moved by 1% of the time
where the time goes in v7:
time: 202 us; the launch traced here: 203 us
  waiting for transfers between devices  119 us (59%)
  starting transfers between devices  38 us (19%)
  between operations  14.3 us (7%)
  local copies, waits for them, and re-layouts  10.9 us (5%)
  Pallas kernels  10.7 us (5%)
  matrix products  6.92 us (3%)
  other arithmetic  3.14 us (2%)
    all_gather x1, waiting for transfers between devices, per_device(): kv = lax.all_gather(kv, ('z', 'x', 'core'), axis=1, tiled=True)  107 us
    ppermute x4, starting transfers between devices, from_behind(): return lax.ppermute(x, axis, pairs)  28 us
    pallas_call x1, Pallas kernels, attend(): pl.pallas_call(functools.partial(attend_kernel, head_count), out_shape=ja...  10.7 us
    ppermute x4, waiting for transfers between devices, from_behind(): return lax.ppermute(x, axis, pairs)  7.9 us
    broadcast_in_dim x1, local copies, waits for them, and re-layouts, per_device(): jnp.broadcast_to(out_weight[None], (shares,) + out_weight.shape)  6.52 us
    all_to_all x1, starting transfers between devices, per_device(): lax.all_to_all(jnp.broadcast_to(out_weight[None], (shares,) + out_weight....  5.91 us
    dot_general x1, matrix products, per_device(): lax.dot_general(weight_all, mine, (((0,), (1,)), ((), ())), preferred_ele...  5.57 us
    all_to_all x1, starting transfers between devices, per_device(): lax.all_to_all(attended.reshape(shares, tokens_dev, attended.shape[1]), (...  4.09 us
  transfers between devices with their start and end apart: 7, of which 4 were waited for; matrix products, arithmetic and copies ran while one was open for 4% of the time, Pallas kernels for 5%

profile of v7, /device:TPU:63, one launch (start us, length us, event | category | flops | bytes accessed | tf_op | source)
XLA Modules:
  0.0 202.6 jit_solution(5668269454810790362)
XLA Ops:
  6.5 1.9 pad_maximum_fusion
  8.4 6.5 %broadcast_in_dim.2 = bf16[4,384,3072]{2,1,0:T(8,128)(2,1)} broadcast(bf16[384,3072]{1,0:T(8,128)(2,1)} %param.17), dimensions={1,2} | broadcast | bytes 11796480 | tf_op jit(solution)/shard_map/broadcast_in_dim | solution.py:137
  14.9 5.9 %all-to-all-start.1 = ((bf16[4,384,3072]{2,1,0:T(8,128)(2,1)}), bf16[4,384,3072]{2,1,0:T(8,128)(2,1)}, u32[]{:S(2)}, u32[]{:S(2)}) async-start(bf16[4,384,3072]{2,1,0:T(8,128)(2,1)} %broadcast_in_dim.2), calls=%async_computation.1 | async-start | bytes 18874368 | tf_op jit(solution)/shard_map/all_to_all | solution.py:136
  20.9 0.7 fusion.13
  22.3 107.2 %all-gather.2.cloned.1.call-done = bf16[2,16384,384]{2,1,0:T(8,128)(2,1)} async-done(((bf16[2,256,384]{2,1,0:T(8,128)(2,1)}), bf16[2,16384,384]{2,1,0:T(8,128)(2,1)}) %all-gather.2.cloned.1.call-update) | async-done | bytes 25165840 | tf_op jit(solution)/shard_map/all_gather | solution.py:130
  129.5 10.7 %shard_map.118 = bf16[256,384]{1,0:T(8,128)(2,1)} custom-call(s32[5]{0:T(128)S(1)} %pad_add_fusion.sp_ref, bf16[256,384]{1,0:T(8,128)(2,1)S(1)} %copy-done.1, bf16[2,8,2048,384]{3,2,1,0:T(8,128)(2,1)} %bitcast.53), custom_call_target="tpu_custom_call" | custom-call | flops 4831838208 | bytes 19267584 | tf_op jit(solution)/shard_map/pallas_call | solution.py:76
  140.3 4.1 %all-to-all-start = ((bf16[4,64,384]{2,1,0:T(8,128)(2,1)}), bf16[4,64,384]{2,1,0:T(8,128)(2,1)S(1)}, u32[]{:S(2)}, u32[]{:S(2)}) async-start(bf16[4,64,384]{2,1,0:T(8,128)(2,1)} %bitcast.5), calls=%async_computation | async-start | bytes 393216 | tf_op jit(solution)/shard_map/all_to_all | solution.py:140
  144.4 3.4 %all-to-all-done = bf16[4,64,384]{2,1,0:T(8,128)(2,1)S(1)} async-done(((bf16[4,64,384]{2,1,0:T(8,128)(2,1)}), bf16[4,64,384]{2,1,0:T(8,128)(2,1)S(1)}, u32[]{:S(2)}, u32[]{:S(2)}) %all-to-all-start) | async-done | bytes 196640 | tf_op jit(solution)/shard_map/all_to_all | solution.py:140
  147.8 5.6 %fusion.18 = (f32[64]{0:T(128)S(1)}, f32[64,3072]{1,0:T(8,128)S(1)}) fusion(bf16[4,384,3072]{2,1,0:T(8,128)(2,1)} %all-to-all-done.1, bf16[4,64,384]{2,1,0:T(8,128)(2,1)S(1)} %all-to-all-done, f32[3072]{0:T(1024)S(1)} %copy-done.3, bf16[64,3072]{1,0:T(8,128)(2,1)S(1)} %copy-done.2), kind=kOutput, calls=%fused_computation.37 | convolution fusion | flops 604766144 | bytes 10825984 | tf_op jit(solution)/shard_map/dot_general | solution.py:144
  153.4 0.3 multiply_reduce_fusion
  153.7 0.3 convolution_convert_fusion
  154.0 0.1 copy.17
  154.2 0.1 copy.18
  154.3 0.1 reshape.105
  154.5 11.6 %collective-permute-start = (bf16[1,1024]{1,0:T(2,128)(2,1)S(1)}, bf16[1,1024]{1,0:T(2,128)(2,1)S(1)}, u32[]{:S(2)}, u32[]{:S(2)}) collective-permute-start(bf16[1,1024]{1,0:T(2,128)(2,1)S(1)} %get-tuple-element.35), channel_id=1, source_target_pairs={{0,1},{1,2},{2,3},{3,4},{4,5},{5,6},{6,7},{7,8},{8,9},{9,10},{10,1... | collective-permute-start | bytes 6152 | tf_op jit(solution)/shard_map/ppermute | solution.py:22
  166.0 1.9 collective-permute-start.1
  168.1 7.1 %collective-permute-done.1 = bf16[1,1024]{1,0:T(2,128)(2,1)S(1)} collective-permute-done((bf16[1,1024]{1,0:T(2,128)(2,1)S(1)}, bf16[1,1024]{1,0:T(2,128)(2,1)S(1)}, u32[]{:S(2)}, u32[]{:S(2)}) %collective-permute-start.1) | collective-permute-done | bytes 2080 | tf_op jit(solution)/shard_map/ppermute | solution.py:22
  175.2 11.5 %collective-permute-start.2 = (bf16[6,1024]{1,0:T(8,128)(2,1)S(1)}, bf16[6,1024]{1,0:T(8,128)(2,1)S(1)}, u32[]{:S(2)}, u32[]{:S(2)}) collective-permute-start(bf16[6,1024]{1,0:T(8,128)(2,1)S(1)} %pad_maximum_fusion.3), channel_id=1, source_target_pairs={{0,64},{1,65},{2,66},{3,67},{4,68},{5,69},{6,70},{7,71},{8,72},{9,... | collective-permute-start | bytes 36872 | tf_op jit(solution)/shard_map/ppermute | solution.py:22
  186.7 3.1 %collective-permute-start.3 = (bf16[6,1024]{1,0:T(8,128)(2,1)S(1)}, bf16[6,1024]{1,0:T(8,128)(2,1)S(1)}, u32[]{:S(2)}, u32[]{:S(2)}) collective-permute-start(bf16[6,1024]{1,0:T(8,128)(2,1)S(1)} %pad_maximum_fusion.3), channel_id=1, source_target_pairs={{0,32},{1,33},{2,34},{3,35},{4,36},{5,37},{6,38},{7,39},{8,40},{9,... | collective-permute-start | bytes 36872 | tf_op jit(solution)/shard_map/ppermute | solution.py:22
  190.2 0.1 copy.40
  190.3 0.1 copy.48
  190.4 0.8 collective-permute-done.3
  191.2 0.1 stack.30
  191.3 0.1 copy.23
  191.5 0.1 stack.31
  191.6 0.1 copy.24
  191.7 0.1 fusion.9
  191.8 0.1 fusion.16
  191.9 0.1 copy.25
  192.1 0.1 copy.26
  192.2 0.1 copy.27
  192.3 0.1 copy.28
  192.4 0.1 copy.29
  192.5 0.1 copy.30
  192.6 0.1 copy.31
  192.7 0.1 copy.32
  192.8 0.1 copy.33
  192.9 0.1 copy.34
  193.0 0.1 copy.35
  193.1 0.1 copy.36
  193.2 0.1 copy.37
  193.3 0.1 copy.41
  193.5 0.1 copy.42
  193.6 0.1 copy.44
  193.7 0.1 copy.45
  193.8 0.1 copy.49
  193.9 0.8 concatenate.115
  194.8 1.0 fusion.2
  (41 shorter events, 0.9 us)
Async XLA Ops:
  6.5 188.2 %copy-start = (bf16[432,512]{1,0:T(8,128)(2,1)S(1)}, bf16[432,512]{1,0:T(8,128)(2,1)}, u32[]{:S(2)}) copy-start(bf16[432,512]{1,0:T(8,128)(2,1)} %param.22) | copy-start | bytes 1327108
  6.5 123.0 %all-gather.2.cloned.1.call-start = ((), (), s32[]{:S(2)}) async-start(), calls=%async_computation.2 | async-start | bytes 25559040 | tf_op jit(solution)/shard_map/all_gather | solution.py:130
  14.9 5.9 %copy-start.5 = (s32[12]{0:T(128)S(1)}, s32[12]{0:T(128)}, u32[]{:S(2)}) copy-start(s32[12]{0:T(128)} %param.15) | copy-start | bytes 148
  14.9 114.6 %copy-start.1 = (bf16[256,384]{1,0:T(8,128)(2,1)S(1)}, bf16[256,384]{1,0:T(8,128)(2,1)}, u32[]{:S(2)}) copy-start(bf16[256,384]{1,0:T(8,128)(2,1)} %q_ref.1) | copy-start | bytes 589828
  14.9 125.3 %all-to-all-start.1 = ((bf16[4,384,3072]{2,1,0:T(8,128)(2,1)}), bf16[4,384,3072]{2,1,0:T(8,128)(2,1)}, u32[]{:S(2)}, u32[]{:S(2)}) async-start(bf16[4,384,3072]{2,1,0:T(8,128)(2,1)} %broadcast_in_dim.2), calls=%async_computation.1 | async-start | bytes 18874368 | tf_op jit(solution)/shard_map/all_to_all | solution.py:136
  129.5 14.8 %copy-start.4 = (f32[3072]{0:T(1024)S(1)}, f32[3072]{0:T(1024)}, u32[]{:S(2)}) copy-start(f32[3072]{0:T(1024)} %param.20) | copy-start | bytes 36868
  129.5 18.3 %copy-start.2 = (bf16[64,3072]{1,0:T(8,128)(2,1)S(1)}, bf16[64,3072]{1,0:T(8,128)(2,1)}, u32[]{:S(2)}) copy-start(bf16[64,3072]{1,0:T(8,128)(2,1)} %param.16) | copy-start | bytes 1179652
  129.5 18.3 %copy-start.3 = (f32[3072]{0:T(1024)S(1)}, f32[3072]{0:T(1024)}, u32[]{:S(2)}) copy-start(f32[3072]{0:T(1024)} %param.18) | copy-start | bytes 36868
  140.2 13.4 %copy-start.6 = (bf16[3072,64]{0,1:T(8,128)(2,1)S(1)}, bf16[3072,64]{0,1:T(8,128)(2,1)}, u32[]{:S(2)}) copy-start(bf16[3072,64]{0,1:T(8,128)(2,1)} %param.21) | copy-start | bytes 1179652
  140.2 13.4 %copy-start.7 = (f32[3072]{0:T(1024)S(1)}, f32[3072]{0:T(1024)}, u32[]{:S(2)}) copy-start(f32[3072]{0:T(1024)} %param.19) | copy-start | bytes 36868
  140.3 7.5 %all-to-all-start = ((bf16[4,64,384]{2,1,0:T(8,128)(2,1)}), bf16[4,64,384]{2,1,0:T(8,128)(2,1)S(1)}, u32[]{:S(2)}, u32[]{:S(2)}) async-start(bf16[4,64,384]{2,1,0:T(8,128)(2,1)} %bitcast.5), calls=%async_computation | async-start | bytes 393216 | tf_op jit(solution)/shard_map/all_to_all | solution.py:140
  144.3 50.4 %copy-start.8 = (f32[512]{0:T(512)S(1)}, f32[512]{0:T(512)}, u32[]{:S(2)}) copy-start(f32[512]{0:T(512)} %param.23) | copy-start | bytes 6148
  154.5 13.6 %collective-permute-start = (bf16[1,1024]{1,0:T(2,128)(2,1)S(1)}, bf16[1,1024]{1,0:T(2,128)(2,1)S(1)}, u32[]{:S(2)}, u32[]{:S(2)}) collective-permute-start(bf16[1,1024]{1,0:T(2,128)(2,1)S(1)} %get-tuple-element.35), channel_id=1, source_target_pairs={{0,1},{1,2},{2,3},{3,4},{4,5},{5,6},{6,7},{7,8},{8,9},{9,10},{10,1... | collective-permute-start | bytes 6152 | tf_op jit(solution)/shard_map/ppermute | solution.py:22
  166.0 9.1 %collective-permute-start.1 = (bf16[1,1024]{1,0:T(2,128)(2,1)S(1)}, bf16[1,1024]{1,0:T(2,128)(2,1)S(1)}, u32[]{:S(2)}, u32[]{:S(2)}) collective-permute-start(bf16[1,1024]{1,0:T(2,128)(2,1)S(1)} %get-tuple-element.36), channel_id=1, source_target_pairs={{1,0},{2,1},{3,2},{4,3},{5,4},{6,5},{7,6},{8,7},{9,8},{10,9},{11,1... | collective-permute-start | bytes 6152 | tf_op jit(solution)/shard_map/ppermute | solution.py:22
  175.2 15.2 %collective-permute-start.2 = (bf16[6,1024]{1,0:T(8,128)(2,1)S(1)}, bf16[6,1024]{1,0:T(8,128)(2,1)S(1)}, u32[]{:S(2)}, u32[]{:S(2)}) collective-permute-start(bf16[6,1024]{1,0:T(8,128)(2,1)S(1)} %pad_maximum_fusion.3), channel_id=1, source_target_pairs={{0,64},{1,65},{2,66},{3,67},{4,68},{5,69},{6,70},{7,71},{8,72},{9,... | collective-permute-start | bytes 36872 | tf_op jit(solution)/shard_map/ppermute | solution.py:22
  186.7 4.5 %collective-permute-start.3 = (bf16[6,1024]{1,0:T(8,128)(2,1)S(1)}, bf16[6,1024]{1,0:T(8,128)(2,1)S(1)}, u32[]{:S(2)}, u32[]{:S(2)}) collective-permute-start(bf16[6,1024]{1,0:T(8,128)(2,1)S(1)} %pad_maximum_fusion.3), channel_id=1, source_target_pairs={{0,32},{1,33},{2,34},{3,35},{4,36},{5,37},{6,38},{7,39},{8,40},{9,... | collective-permute-start | bytes 36872 | tf_op jit(solution)/shard_map/ppermute | solution.py:22
Sparse Core Ops, SparseCore 0:
  10.0 119.4 all-gather.1
